TPU v7x, 256 devices: a whole 4x4x8 slice. The times are simulated.
256 devices in a mesh: row: 4 (over y), col: 4 (over x), dp: 16 (over z, core).
Axes of the slice: x: 4, y: 4, z: 8, core: 2. Of those that a mesh axis runs over, the one named last changes fastest.
Arguments:
- hidden_states: bfloat16 [16384, 1536], P(('dp', 'row'), 'col'), may hold values from -18 to 18
- w_query: bfloat16 [1536, 1536], P('col', 'row'), may hold values from -0.102062073 to 0.102062073
- w_key_value: bfloat16 [1536, 512], P('col'), may hold values from -0.102062073 to 0.102062073
- adapter_down: bfloat16 [1024, 1536, 16], P('dp', 'col'), may hold values from -0.15625 to 0.15625
- adapter_up: bfloat16 [1024, 16, 1536], P('dp', None, 'row'), may hold values from -1.5 to 1.5
- req_lengths: int32 [16, 8], replicated, may hold values from 1 to 160, 960 in all within a row
- req_adapter: int32 [16, 8], replicated, may hold values from 0 to 1023, as said below
Outputs:
- attention: bfloat16 [16384, 1536], P(('dp', 'col'), 'row')
- kv_cache: bfloat16 [16384, 512], P(('dp', 'col'))
Inputs may be any that keep to these rules, and one draw needn't show every extreme that they name: `req_lengths`: the lengths of one block sum to 960, and each block has a request of exactly 160 tokens. `req_adapter`: adapters k * 64 to (k + 1) * 64 - 1 are those of index k of dp; the requests of one block use adapters of one index of dp at most 1 times, and some index of dp is used exactly that often by every block.
All inputs are finite; a program needn't handle non-finite values.
Results may differ from a plain program's by a relative error of at most 0.0072.
Values may be sent and summed in bfloat16 or wider, within the bound.
No kernel may reach another device: no remote copies, remote signals or barrier semaphores. Data moves between devices by JAX's collectives and lax.ppermute only.
A program may use at most 128 MiB of HBM per device.

v0:
```python
import math

import jax
import jax.numpy as jnp
from jax import lax
from jax.sharding import PartitionSpec as P

HEAD_DIM = 128
MOST_LEN = 160


masked_score = -1e30


def block_layout(lengths_row, block_len):
    prefix_len = block_len - jnp.sum(lengths_row)
    ends_at = jnp.cumsum(lengths_row) + prefix_len
    starts = ends_at - lengths_row
    positions = jnp.arange(block_len, dtype=jnp.int32)
    segment = jnp.sum((positions[:, None] >= starts[None, :]).astype(jnp.int32), axis=1)
    return (starts, segment, positions)


def slot_numbers(holders):
    request_total = holders.shape[0]
    ordering = jnp.arange(request_total, dtype=jnp.int32)
    earlier = ordering[None, :] < ordering[:, None]
    same_holder = holders[:, None] == holders[None, :]
    return jnp.sum((earlier & same_holder).astype(jnp.int32), axis=1)


def make_attend(query_rows, segment, first_row, kv_group, head_size, kv_half):
    own_rows = query_rows.shape[0]
    heads_here = query_rows.shape[1] // head_size
    query_heads = query_rows.reshape(own_rows, heads_here, head_size)
    query_pos = first_row + jnp.arange(own_rows, dtype=jnp.int32)
    query_seg = lax.dynamic_slice_in_dim(segment, first_row, own_rows, 0)
    score_scale = 1.0 / math.sqrt(head_size)

    def attend(state_in, key_block, key_start):
        running_max, running_sum, running_out = state_in
        block_size = key_block.shape[0]
        key_rows = lax.dynamic_slice_in_dim(key_block, kv_group * head_size, head_size, 1)
        values = lax.dynamic_slice_in_dim(key_block, kv_half + kv_group * head_size, head_size, 1)
        key_pos = jnp.arange(block_size, dtype=jnp.int32)
        allowed = (key_pos[None, :] <= query_pos[:, None]) & (
            (segment[None, :] == query_seg[:, None]) | (segment[None, :] == 0)
        )
        scores = (
            jnp.einsum("qhd,kd->hqk", query_heads, key_rows, preferred_element_type=jnp.float32)
            * score_scale
        )
        scores = jnp.where(allowed[None], scores, masked_score)
        new_max = jnp.maximum(running_max, jnp.max(scores, axis=2))
        weights = jnp.where(allowed[None], jnp.exp(scores - new_max[:, :, None]), 0.0)
        running_sum = jnp.sum(weights, axis=2)
        running_out = jnp.einsum(
            "hqk,kd->hqd", weights.astype(jnp.bfloat16), values, preferred_element_type=jnp.float32
        )
        return (new_max, running_sum, running_out)

    initial = (
        jnp.full((heads_here, own_rows), masked_score, jnp.float32),
        jnp.zeros((heads_here, own_rows), jnp.float32),
        jnp.zeros((heads_here, own_rows, head_size), jnp.float32),
    )
    return (attend, initial)


def body(hidden_states, w_query, w_key_value, adapter_down, adapter_up, req_lengths, req_adapter):
    dp_size = lax.axis_size("dp")
    block_index = lax.axis_index("dp")
    col_index = lax.axis_index("col")
    row_index = lax.axis_index("row")
    gathered = lax.all_gather(hidden_states, "row", axis=0, tiled=True)
    block_len = gathered.shape[0]
    query_cols = w_query.shape[1]
    kv_cols = w_key_value.shape[1]
    kv_half = kv_cols // 2
    head_size = HEAD_DIM
    heads_here = query_cols // head_size
    heads_total = heads_here * lax.axis_size("row")
    kv_heads = kv_half // head_size
    kv_group = row_index * heads_here // (heads_total // kv_heads)
    own_rows = block_len // lax.axis_size("col")
    first_row = col_index * own_rows
    held_sets = adapter_down.shape[0]
    width_here = adapter_down.shape[1]
    rank_size = adapter_down.shape[2]
    lengths_row = req_lengths[block_index]
    adapters_row = req_adapter[block_index]
    requests = lengths_row.shape[0]
    starts, segment, positions = block_layout(lengths_row, block_len)
    request_of = jnp.clip(segment - 1, 0, requests - 1)
    in_request = segment > 0
    holders = adapters_row // held_sets
    slot_of = slot_numbers(holders)
    per_holder = (requests + dp_size - 1) // dp_size
    longest = MOST_LEN
    target_ids = jnp.arange(dp_size, dtype=jnp.int32)[:, None, None]
    slot_ids = jnp.arange(per_holder, dtype=jnp.int32)[None, :, None]
    pairing = (holders[None, None, :] == target_ids) & (slot_of[None, None, :] == slot_ids)
    pair_int = pairing.astype(jnp.int32)
    slot_start = jnp.sum(pair_int * starts[None, None, :], axis=2)
    slot_len = jnp.sum(pair_int * lengths_row[None, None, :], axis=2)
    slot_adapter = jnp.where(
        jnp.any(pairing, axis=2),
        jnp.sum(pair_int * (adapters_row % held_sets)[None, None, :], axis=2),
        -1,
    )
    offsets = jnp.arange(longest, dtype=jnp.int32)
    token_at = slot_start[:, :, None] + offsets[None, None, :]
    live_rows = offsets[None, None, :] < slot_len[:, :, None]
    outgoing = jnp.where(
        live_rows[..., None],
        gathered[jnp.clip(token_at, 0, block_len - 1)],
        jnp.zeros((), gathered.dtype),
    )
    flat_down = jnp.transpose(adapter_down, (1, 0, 2)).reshape(width_here, held_sets * rank_size)
    flat_up = adapter_up.reshape(held_sets * rank_size, query_cols).astype(jnp.float32)
    rank_owner = jnp.arange(held_sets * rank_size, dtype=jnp.int32) // rank_size
    sent_rows = lax.all_to_all(outgoing, "dp", split_axis=0, concat_axis=0, tiled=True)
    sent_ids = lax.all_to_all(
        slot_adapter.astype(jnp.bfloat16), "dp", split_axis=0, concat_axis=0, tiled=True
    )
    reduced = jnp.einsum("nkld,da->nkla", sent_rows, flat_down, preferred_element_type=jnp.float32)
    kept_cols = rank_owner[None, None, :] == sent_ids.astype(jnp.int32)[:, :, None]
    reduced = jnp.where(kept_cols[:, :, None, :], reduced, 0.0)
    adapter_part = jnp.einsum("nkla,af->nklf", reduced, flat_up, precision=lax.Precision.HIGHEST)
    returned = lax.all_to_all(adapter_part, "dp", split_axis=0, concat_axis=0, tiled=True)
    flat_index = (holders[request_of] * per_holder + slot_of[request_of]) * longest + jnp.clip(
        positions - starts[request_of], 0, longest - 1
    )
    adapter_term = returned.reshape(-1, query_cols)[flat_index]
    adapter_term = jnp.where(in_request[:, None], adapter_term, 0.0)
    both_weights = jnp.concatenate([w_query, w_key_value], axis=1)
    partial_value = jnp.dot(gathered, both_weights, preferred_element_type=jnp.float32)
    summed = lax.psum_scatter(
        partial_value
        + jnp.concatenate(
            [adapter_term, jnp.zeros((own_rows * lax.axis_size("col"), kv_cols), jnp.float32)],
            axis=1,
        ),
        "col",
        scatter_dimension=0,
        tiled=True,
    )
    query_rows = summed[:, :query_cols].astype(jnp.bfloat16)
    kv_cache = summed[:, query_cols:].astype(jnp.bfloat16)
    attend, initial = make_attend(query_rows, segment, first_row, kv_group, head_size, kv_half)
    running_max, running_sum, running_out = attend(
        initial, lax.all_gather(kv_cache, "col", axis=0, tiled=True), jnp.int32(0)
    )
    attention = (running_out / running_sum[:, :, None]).astype(jnp.bfloat16)
    attention = jnp.transpose(attention, (1, 0, 2)).reshape(own_rows, query_cols)
    return (attention, kv_cache)


def solution(mesh):
    return jax.shard_map(
        body,
        mesh=mesh,
        in_specs=(
            P(("dp", "row"), "col"),
            P("col", "row"),
            P("col", None),
            P("dp", "col", None),
            P("dp", None, "row"),
            P(),
            P(),
        ),
        out_specs=(P(("dp", "col"), "row"), P(("dp", "col"), None)),
        check_vma=False,
    )
```

profile of v0, /device:TPU:160, one launch (start us, length us, event | category | flops | bytes accessed | tf_op | source)
XLA Modules:
  0.0 301.7 jit_solution(6985747026854632109)
XLA Ops:
  7.2 0.0 copy-start
  7.2 1.5 fusion.34
  8.7 0.1 copy.62
  8.8 0.2 reduce-window.4
  9.0 0.0 copy-start.6
  9.0 0.2 convert_reduce_fusion.2
  9.1 0.5 copy-done.8
  9.6 0.1 fusion.39
  10.4 0.0 copy-start.4
  10.4 0.5 copy-done.4
  10.9 0.1 select_reduce_fusion.2
  11.0 0.7 copy.46
  11.7 6.8 %all-to-all-start = ((bf16[16,1,1]{2,1,0:T(2,128)(2,1)}), bf16[16,1,1]{2,1,0:T(2,128)(2,1)}, u32[]{:S(2)}, u32[]{:S(2)}) async-start(bf16[16,1,1]{2,1,0:T(2,128)(2,1)} %copy.46), calls=%async_computation | async-start | bytes 16384 | tf_op jit(solution)/shard_map/all_to_all | solution.py:123
  18.5 0.0 copy-done.10
  18.5 0.0 copy-done.12
  18.5 0.0 copy-done.6
  18.5 0.1 compare_select_fusion
  18.6 0.1 reshape.714
  18.7 14.2 %all_gather.6 = bf16[1024,384]{1,0:T(8,128)(2,1)S(1)} all-gather(bf16[256,384]{1,0:T(8,128)(2,1)} %param.7), channel_id=1, replica_groups=mesh['row'=4,'col'=4,'dp'=16] {'row'}, dimensions={0}, use_global_device_ids=true | all-gather | bytes 983040 | tf_op jit(solution)/shard_map/all_gather | solution.py:75
  32.9 0.1 iota_compare_fusion.2
  33.0 7.5 %gather_fusion = bf16[2560,384]{1,0:T(8,128)(2,1)S(1)} fusion(bf16[1024,384]{1,0:T(8,128)(2,1)S(1)} %all_gather.6, s32[3072]{0:T(1024)S(1)} %pad_clamp_fusion), kind=kCustom, calls=%fused_computation | custom fusion | bytes 3942400 | tf_op jit(solution)/shard_map/gather | solution.py:116
  40.5 1.5 broadcast_select_fusion
  42.0 0.0 all-to-all-done
  42.0 7.2 %all-to-all-start.1 = ((bf16[16,1,160,384]{3,2,1,0:T(8,128)(2,1)}), bf16[16,1,160,384]{3,2,1,0:T(8,128)(2,1)S(1)}, u32[]{:S(2)}, u32[]{:S(2)}) async-start(bf16[16,1,160,384]{3,2,1,0:T(8,128)(2,1)} %broadcast_select_fusion), calls=%async_computation.1 | async-start | bytes 3932160 | tf_op jit(solution)/shard_map/all_to_all | solution.py:122
  49.3 1.1 convert_reduce_fusion.1
  50.4 0.1 broadcast_compare_fusion
  50.4 43.6 %all-to-all-done.1 = bf16[16,1,160,384]{3,2,1,0:T(8,128)(2,1)S(1)} async-done(((bf16[16,1,160,384]{3,2,1,0:T(8,128)(2,1)}), bf16[16,1,160,384]{3,2,1,0:T(8,128)(2,1)S(1)}, u32[]{:S(2)}, u32[]{:S(2)}) %all-to-all-start.1) | async-done | bytes 1966112 | tf_op jit(solution)/shard_map/all_to_all | solution.py:122
  94.0 0.0 copy-done
  94.0 3.0 fusion.10
  97.0 0.0 copy-done.1
  97.0 10.3 %fusion.7 = f32[16,1,160,384]{3,2,1,0:T(8,128)} fusion(bf16[1024,384,1]{1,0,2:T(8,128)(2,1)S(1)} %bitcast.109, f32[16,160,1024]{2,1,0:T(8,128)S(1)} %fusion.10, pred[16,1024]{1,0:T(8,128)(4,1)S(1)} %broadcast_compare_fusion), kind=kOutput, calls=%fused_computation.12 | convolution fusion | flops 12082216960 | bytes 15220736 | tf_op jit(solution)/shard_map/nkla,af->nklf/dot_general | solution.py:129
  107.3 0.0 copy-start.13
  107.4 6.4 %all-to-all-start.2 = ((f32[16,1,160,384]{3,2,1,0:T(8,128)}), f32[16,1,160,384]{3,2,1,0:T(8,128)}, u32[]{:S(2)}, u32[]{:S(2)}) async-start(f32[16,1,160,384]{3,2,1,0:T(8,128)} %fusion.7), calls=%async_computation.2 | async-start | bytes 7864320 | tf_op jit(solution)/shard_map/all_to_all | solution.py:130
  113.7 0.2 reduce-scatter.2.cloned.1.call-start
  113.9 0.0 copy-done.5
  113.9 0.7 fusion.52
  114.6 0.0 copy-done.9
  114.6 0.7 fusion.54
  115.3 0.7 fusion.53
  116.0 0.1 convert_reduce_fusion
  116.1 4.1 %select_select_fusion.2 = s32[1024,1]{0,1:T(1,128)S(1)} fusion(s32[]{:T(128)} %bitcast.20, s32[]{:T(128)} %bitcast.21, s32[]{:T(128)} %bitcast.22, s32[]{:T(128)} %bitcast.23, s32[]{:T(128)} %bitcast.24, s32[]{:T(128)} %bitcast.26, s32[]{:T(128)} %bitcast.25, s32[1024,1]{0,1:T(1,128)S(1)} %bitcast.113), kind=kLoop, calls=%fused_computation.56 | loop fusion | flops 15360 | bytes 8220 | tf_op jit(solution)/shard_map/gather | solution.py:131
  120.2 9.0 %select_select_fusion = (s32[1024,1]{0,1:T(1,128)S(1)}, s32[1024,1]{0,1:T(1,128)S(1)}) fusion(s32[]{:T(128)} %bitcast.39, s32[]{:T(128)} %bitcast.40, s32[]{:T(128)} %bitcast.41, s32[]{:T(128)} %bitcast.42, s32[]{:T(128)} %bitcast.43, s32[]{:T(128)} %bitcast.45, s32[]{:T(128)} %bitcast.44, s32[1024,1]{0,1:T(1,128)S(1)} %bitcast.114, s32[]{:T(128)} %bitcast.35, ...), kind=kLoop, calls=%fused_computation.54 | loop fusion | flops 21504 | bytes 12344 | tf_op jit(solution)/shard_map/gather | solution.py:132
  129.3 1.9 broadcast_select_fusion.2
  131.2 69.6 %all-to-all-done.2 = f32[16,1,160,384]{3,2,1,0:T(8,128)} async-done(((f32[16,1,160,384]{3,2,1,0:T(8,128)}), f32[16,1,160,384]{3,2,1,0:T(8,128)}, u32[]{:S(2)}, u32[]{:S(2)}) %all-to-all-start.2) | async-done | bytes 3932192 | tf_op jit(solution)/shard_map/all_to_all | solution.py:130
  200.8 7.1 %gather_fusion.1 = f32[1024,384]{1,0:T(8,128)} fusion(f32[2560,384]{1,0:T(8,128)} %bitcast.17, s32[1024]{0:T(1024)S(1)} %broadcast_clamp_fusion), kind=kCustom, calls=%fused_computation.1 | custom fusion | bytes 3149824 | tf_op jit(solution)/shard_map/gather | solution.py:134
  207.9 1.9 copy.50
  209.8 0.0 copy-start.3
  209.8 0.2 broadcast_select_fusion.1
  210.0 0.8 copy-done.3
  210.8 3.0 bitcast_add_fusion
  213.7 0.0 reduce-scatter.2.cloned.1.call-update
  213.8 0.0 all-gather.2.cloned.1.call-start
  213.8 45.9 %reduce-scatter.2.cloned.1.call-done = f32[256,896]{0,1:T(8,128)} async-done(((f32[1024,896]{0,1:T(8,128)}), f32[256,896]{0,1:T(8,128)}) %reduce-scatter.2.cloned.1.call-update) | async-done | bytes 917520 | tf_op jit(solution)/shard_map/reduce_scatter | solution.py:138
  259.8 1.2 convert.5
  261.0 0.7 slice.41
  261.7 0.0 all-gather.2.cloned.1.call-update
  261.8 0.1 dynamic_slice.18
  261.9 0.8 fusion.18
  262.7 1.8 copy.55
  264.5 25.1 %all-gather.2.cloned.1.call-done = bf16[1024,512]{0,1:T(8,128)(2,1)} async-done(((bf16[256,512]{0,1:T(8,128)(2,1)}), bf16[1024,512]{0,1:T(8,128)(2,1)}) %all-gather.2.cloned.1.call-update) | async-done | bytes 1048592 | tf_op jit(solution)/shard_map/all_gather | solution.py:152
  289.6 1.7 fusion.4
  291.3 0.8 fusion.5
  292.1 1.9 fusion.22
  294.1 0.8 copy.54
  (28 shorter events, 0.2 us)
Async XLA Ops:
  7.2 86.9 %copy-start = (bf16[64,384,16]{1,2,0:T(8,128)(2,1)S(1)}, bf16[64,384,16]{1,2,0:T(8,128)(2,1)}, u32[]{:S(2)}) copy-start(bf16[64,384,16]{1,2,0:T(8,128)(2,1)} %param.10) | copy-start | bytes 2359300
  8.8 9.7 %copy-start.10 = (s32[1,8]{1,0:T(1,128)}, s32[1,8]{1,0:T(1,128)S(1)}, u32[]{:S(2)}) copy-start(s32[1,8]{1,0:T(1,128)S(1)} %copy.62) | copy-start | bytes 100
  8.9 9.6 %copy-start.12 = (s32[8,1]{0,1:T(1,128)}, s32[8,1]{0,1:T(1,128)S(1)}, u32[]{:S(2)}) copy-start(s32[8,1]{0,1:T(1,128)S(1)} %reduce-window.4) | copy-start | bytes 100
  9.0 9.6 %copy-start.6 = (s32[8]{0:T(128)}, s32[8]{0:T(128)S(1)}, u32[]{:S(2)}) copy-start(s32[8]{0:T(128)S(1)} %get-tuple-element.49) | copy-start | bytes 100
  9.1 0.5 copy-start.8
  10.4 0.5 copy-start.4
  11.7 30.3 %all-to-all-start = ((bf16[16,1,1]{2,1,0:T(2,128)(2,1)}), bf16[16,1,1]{2,1,0:T(2,128)(2,1)}, u32[]{:S(2)}, u32[]{:S(2)}) async-start(bf16[16,1,1]{2,1,0:T(2,128)(2,1)} %copy.46), calls=%async_computation | async-start | bytes 16384 | tf_op jit(solution)/shard_map/all_to_all | solution.py:123
  42.0 52.0 %all-to-all-start.1 = ((bf16[16,1,160,384]{3,2,1,0:T(8,128)(2,1)}), bf16[16,1,160,384]{3,2,1,0:T(8,128)(2,1)S(1)}, u32[]{:S(2)}, u32[]{:S(2)}) async-start(bf16[16,1,160,384]{3,2,1,0:T(8,128)(2,1)} %broadcast_select_fusion), calls=%async_computation.1 | async-start | bytes 3932160 | tf_op jit(solution)/shard_map/all_to_all | solution.py:122
  94.0 3.0 copy-start.1
  107.3 6.6 %copy-start.5 = (s32[8]{0:T(128)S(1)}, s32[8]{0:T(128)}, u32[]{:S(2)}) copy-start(s32[8]{0:T(128)} %copy-done.4) | copy-start | bytes 100
  107.3 7.3 %copy-start.9 = (s32[8]{0:T(128)S(1)}, s32[8]{0:T(128)}, u32[]{:S(2)}) copy-start(s32[8]{0:T(128)} %copy-done.8) | copy-start | bytes 100
  107.3 8.0 %copy-start.7 = (s32[8]{0:T(128)S(1)}, s32[8]{0:T(128)}, u32[]{:S(2)}) copy-start(s32[8]{0:T(128)} %copy-done.6) | copy-start | bytes 100
  107.3 8.6 %copy-start.11 = (s32[1,8]{1,0:T(1,128)S(1)}, s32[1,8]{1,0:T(1,128)}, u32[]{:S(2)}) copy-start(s32[1,8]{1,0:T(1,128)} %copy-done.10) | copy-start | bytes 100
  107.3 8.6 %copy-start.13 = (s32[8,1]{0,1:T(1,128)S(1)}, s32[8,1]{0,1:T(1,128)}, u32[]{:S(2)}) copy-start(s32[8,1]{0,1:T(1,128)} %copy-done.12) | copy-start | bytes 100
  107.4 93.4 %all-to-all-start.2 = ((f32[16,1,160,384]{3,2,1,0:T(8,128)}), f32[16,1,160,384]{3,2,1,0:T(8,128)}, u32[]{:S(2)}, u32[]{:S(2)}) async-start(f32[16,1,160,384]{3,2,1,0:T(8,128)} %fusion.7), calls=%async_computation.2 | async-start | bytes 7864320 | tf_op jit(solution)/shard_map/all_to_all | solution.py:130
  113.7 146.1 %reduce-scatter.2.cloned.1.call-start = ((), (), s32[]{:S(2)}) async-start(), calls=%async_computation.4 | async-start | bytes 4587520 | tf_op jit(solution)/shard_map/reduce_scatter | solution.py:138
  207.9 2.1 copy-start.2
  209.8 1.0 copy-start.3
  213.8 75.8 %all-gather.2.cloned.1.call-start = ((), (), s32[]{:S(2)}) async-start(), calls=%async_computation.5 | async-start | bytes 1310720 | tf_op jit(solution)/shard_map/all_gather | solution.py:152
Sparse Core Ops, SparseCore 0:
  213.9 45.8 reduce-scatter.1
  261.9 27.6 all-gather.1
where the time goes:
time: 304 us; the launch traced here: 302 us
  waiting for transfers between devices  184 us (61%)
  local copies, waits for them, and re-layouts  24.7 us (8%)
  other arithmetic  23.1 us (8%)
  starting transfers between devices  20.6 us (7%)
  matrix products  19.9 us (7%)
  between operations  15 us (5%)
  blocking collectives  14.2 us (5%)
    all_to_all x1, waiting for transfers between devices, body(): lax.all_to_all(adapter_part, 'dp', split_axis=0, concat_axis=0, tiled=True)  69.6 us
    reduce_scatter x1, waiting for transfers between devices, body(): lax.psum_scatter(partial_value + jnp.concatenate([adapter_term, jnp.zeros...  45.9 us
    all_to_all x1, waiting for transfers between devices, body(): lax.all_to_all(outgoing, 'dp', split_axis=0, concat_axis=0, tiled=True)  43.6 us
    all_gather x1, waiting for transfers between devices, body(): lax.all_gather(kv_cache, 'col', axis=0, tiled=True)  25.1 us
    all_gather x1, blocking collectives, body(): gathered = lax.all_gather(hidden_states, 'row', axis=0, tiled=True)  14.2 us
    gather x2, other arithmetic, body(): starts[request_of]  10.9 us
    dot_general x1, matrix products, body(): jnp.einsum('nkla,af->nklf', reduced, flat_up, precision=lax.Precision.HIG...  10.3 us
    gather x2, local copies, waits for them, and re-layouts, body(): adapter_term = returned.reshape(-1, query_cols)[flat_index]  9.02 us
  transfers between devices with their start and end apart: 5, of which 4 were waited for; matrix products, arithmetic and copies ran while one was open for 10% of the time, Pallas kernels for 0%

commit v1 on v0

--- a/solution.py
+++ b/solution.py
@@ -94,45 +94,20 @@
     request_of = jnp.clip(segment - 1, 0, requests - 1)
     in_request = segment > 0
     holders = adapters_row // held_sets
-    slot_of = slot_numbers(holders)
-    per_holder = (requests + dp_size - 1) // dp_size
-    longest = MOST_LEN
-    target_ids = jnp.arange(dp_size, dtype=jnp.int32)[:, None, None]
-    slot_ids = jnp.arange(per_holder, dtype=jnp.int32)[None, :, None]
-    pairing = (holders[None, None, :] == target_ids) & (slot_of[None, None, :] == slot_ids)
-    pair_int = pairing.astype(jnp.int32)
-    slot_start = jnp.sum(pair_int * starts[None, None, :], axis=2)
-    slot_len = jnp.sum(pair_int * lengths_row[None, None, :], axis=2)
-    slot_adapter = jnp.where(
-        jnp.any(pairing, axis=2),
-        jnp.sum(pair_int * (adapters_row % held_sets)[None, None, :], axis=2),
-        -1,
-    )
-    offsets = jnp.arange(longest, dtype=jnp.int32)
-    token_at = slot_start[:, :, None] + offsets[None, None, :]
-    live_rows = offsets[None, None, :] < slot_len[:, :, None]
-    outgoing = jnp.where(
-        live_rows[..., None],
-        gathered[jnp.clip(token_at, 0, block_len - 1)],
-        jnp.zeros((), gathered.dtype),
-    )
-    flat_down = jnp.transpose(adapter_down, (1, 0, 2)).reshape(width_here, held_sets * rank_size)
-    flat_up = adapter_up.reshape(held_sets * rank_size, query_cols).astype(jnp.float32)
-    rank_owner = jnp.arange(held_sets * rank_size, dtype=jnp.int32) // rank_size
-    sent_rows = lax.all_to_all(outgoing, "dp", split_axis=0, concat_axis=0, tiled=True)
-    sent_ids = lax.all_to_all(
-        slot_adapter.astype(jnp.bfloat16), "dp", split_axis=0, concat_axis=0, tiled=True
-    )
-    reduced = jnp.einsum("nkld,da->nkla", sent_rows, flat_down, preferred_element_type=jnp.float32)
-    kept_cols = rank_owner[None, None, :] == sent_ids.astype(jnp.int32)[:, :, None]
-    reduced = jnp.where(kept_cols[:, :, None, :], reduced, 0.0)
-    adapter_part = jnp.einsum("nkla,af->nklf", reduced, flat_up, precision=lax.Precision.HIGHEST)
-    returned = lax.all_to_all(adapter_part, "dp", split_axis=0, concat_axis=0, tiled=True)
-    flat_index = (holders[request_of] * per_holder + slot_of[request_of]) * longest + jnp.clip(
-        positions - starts[request_of], 0, longest - 1
-    )
-    adapter_term = returned.reshape(-1, query_cols)[flat_index]
-    adapter_term = jnp.where(in_request[:, None], adapter_term, 0.0)
+    wanted_from_me = (req_adapter // held_sets) == block_index
+    local_pick = jnp.sum(jnp.where(wanted_from_me, req_adapter % held_sets, 0), axis=1)
+    down_pick = jnp.transpose(jnp.take(adapter_down, local_pick, axis=0), (0, 2, 1))
+    up_pick = jnp.take(adapter_up, local_pick, axis=0)
+    outgoing = jnp.concatenate([down_pick, up_pick], axis=1)
+    incoming = lax.all_to_all(outgoing, "dp", split_axis=0, concat_axis=0, tiled=True)
+    flat_down = incoming[:, :rank_size, :].reshape(dp_size * rank_size, width_here).T
+    flat_up = incoming[:, rank_size:, :].reshape(dp_size * rank_size, query_cols).astype(jnp.float32)
+    rank_owner = jnp.arange(dp_size * rank_size, dtype=jnp.int32) // rank_size
+    reduced = jnp.dot(gathered, flat_down, preferred_element_type=jnp.float32)
+    token_holder = jnp.where(in_request, holders[request_of], -1)
+    kept_cols = rank_owner[None, :] == token_holder[:, None]
+    reduced = jnp.where(kept_cols, reduced, 0.0)
+    adapter_term = jnp.dot(reduced, flat_up, precision=lax.Precision.HIGHEST)
     both_weights = jnp.concatenate([w_query, w_key_value], axis=1)
     partial_value = jnp.dot(gathered, both_weights, preferred_element_type=jnp.float32)
     summed = lax.psum_scatter(

time: 304 us -> 136 us (0.45)
  waiting for transfers between devices: 184 us -> 71.9 us
  local copies, waits for them, and re-layouts: 24.7 us -> 6.81 us
  starting transfers between devices: 20.6 us -> 6.85 us
  other arithmetic: 23.1 us -> 10.8 us
  matrix products: 19.9 us -> 7.95 us
    all_to_all x2 -> x0, waiting for transfers between devices: 69.6 us -> none  [the longest x1 69.6 us: body(): lax.all_to_all(adapter_part, 'dp', split_axis=0, concat_axis=0, tiled=True)]
    all_to_all x1, waiting for transfers between devices: 43.6 us -> 0.01 us  [body(): lax.all_to_all(outgoing, 'dp', split_axis=0, concat_axis=0, tiled=True)]
    gather x6 -> x3, local copies, waits for them, and re-layouts: 18.5 us -> 3.01 us  [the longest x1 1.73 us: body(): jnp.take(adapter_down, local_pick, axis=0)]
    all_to_all x2 -> x0, starting transfers between devices: 13.1 us -> none  [the longest x1 6.77 us: body(): lax.all_to_all(slot_adapter.astype(jnp.bfloat16), 'dp', split_axis=0, con...]
    dot_general x2, matrix products: 13.3 us -> 1.35 us  [the longest x1 0.88 us: body(): adapter_term = jnp.dot(reduced, flat_up, precision=lax.Precision.HIGHEST)]
    gather x6 -> x3, other arithmetic: 15 us -> 4.56 us  [the longest x2 4.55 us: body(): token_holder = jnp.where(in_request, holders[request_of], -1)]
  transfers between devices with their start and end apart: 5 -> 3, of which waited for: 4 -> 2; matrix products, arithmetic and copies ran while one was open for 10% -> 7% of each run, Pallas kernels for 0% -> 0%
where the time goes in v1:
time: 136 us; the launch traced here: 134 us
  waiting for transfers between devices  71.9 us (53%)
  between operations  15 us (11%)
  blocking collectives  14.2 us (10%)
  other arithmetic  10.8 us (8%)
  matrix products  7.95 us (6%)
  starting transfers between devices  6.85 us (5%)
  local copies, waits for them, and re-layouts  6.81 us (5%)
    reduce_scatter x1, waiting for transfers between devices, body(): lax.psum_scatter(partial_value + jnp.concatenate([adapter_term, jnp.zeros...  46.8 us
    all_gather x1, waiting for transfers between devices, body(): lax.all_gather(kv_cache, 'col', axis=0, tiled=True)  25.1 us
    all_gather x1, blocking collectives, body(): gathered = lax.all_gather(hidden_states, 'row', axis=0, tiled=True)  14.2 us
    all_to_all x1, starting transfers between devices, body(): lax.all_to_all(outgoing, 'dp', split_axis=0, concat_axis=0, tiled=True)  6.77 us
    gather x2, other arithmetic, body(): token_holder = jnp.where(in_request, holders[request_of], -1)  4.55 us
    dot_general x1, matrix products, body(): jnp.dot(gathered, both_weights, preferred_element_type=jnp.float32)  2.98 us
    unnamed x14, local copies, waits for them, and re-layouts  2.93 us
  transfers between devices with their start and end apart: 3, of which 2 were waited for; matrix products, arithmetic and copies ran while one was open for 7% of the time, Pallas kernels for 0%

profile of v1, /device:TPU:160, one launch (start us, length us, event | category | flops | bytes accessed | tf_op | source)
XLA Modules:
  0.0 133.5 jit_solution(6287286871601719198)
XLA Ops:
  7.2 0.0 copy-start
  7.2 0.0 copy-start.4
  7.2 0.0 copy-start.5
  7.2 0.0 copy-start.3
  7.2 0.8 fusion.27
  8.0 0.3 copy-done
  8.3 0.6 gather_fusion.1
  8.9 1.7 %gather_fusion = bf16[16,384,16]{1,2,0:T(8,128)(2,1)S(1)} fusion(bf16[64,384,16]{1,2,0:T(8,128)(2,1)} %param.10, s32[1024]{0:T(1024)S(1)} %pad_clamp_fusion), kind=kCustom, calls=%fused_computation | custom fusion | bytes 393280 | tf_op jit(solution)/shard_map/jit(_take)/gather | solution.py:99
  10.6 0.1 broadcast_select_fusion
  10.7 0.1 select_bitcast_fusion
  10.9 0.8 pad_maximum_fusion
  11.6 6.8 %all-to-all-start = ((bf16[16,32,384]{2,1,0:T(8,128)(2,1)}), bf16[16,32,384]{2,1,0:T(8,128)(2,1)S(1)}, u32[]{:S(2)}, u32[]{:S(2)}) async-start(bf16[16,32,384]{2,1,0:T(8,128)(2,1)} %pad_maximum_fusion), calls=%async_computation | async-start | bytes 786432 | tf_op jit(solution)/shard_map/all_to_all | solution.py:102
  18.4 0.0 reduce-scatter.2.cloned.1.call-start
  18.5 0.0 copy-done.4
  18.5 0.0 copy-done.5
  18.5 0.7 fusion.37
  19.9 0.1 subtract_reduce_fusion
  20.0 0.1 convert_reduce_fusion
  20.1 0.7 fusion.39
  20.8 4.5 %compare_select_fusion.1 = s32[1024,1]{0,1:T(1,128)S(1)} fusion(s32[]{:T(128)} %bitcast.3, s32[]{:T(128)} %bitcast.4, s32[]{:T(128)} %bitcast.5, s32[]{:T(128)} %bitcast.6, s32[]{:T(128)} %bitcast.7, s32[]{:T(128)} %bitcast.9, s32[]{:T(128)} %bitcast.8, s32[1024,1]{0,1:T(1,128)S(1)} %bitcast.69), kind=kLoop, calls=%fused_computation.32 | loop fusion | flops 15360 | bytes 8220 | tf_op jit(solution)/shard_map/gather | solution.py:107
  25.4 0.7 select_select_fusion
  26.0 0.0 copy-done.3
  26.1 0.0 copy-start.1
  26.1 0.0 copy-start.2
  26.1 14.2 %all_gather.6 = bf16[1024,384]{1,0:T(8,128)(2,1)S(1)} all-gather(bf16[256,384]{1,0:T(8,128)(2,1)S(1)} %copy-done.3), channel_id=1, replica_groups=mesh['row'=4,'col'=4,'dp'=16] {'row'}, dimensions={0}, use_global_device_ids=true | all-gather | bytes 983040 | tf_op jit(solution)/shard_map/all_gather | solution.py:75
  40.2 0.0 all-to-all-done
  40.3 0.5 fusion.6
  40.8 0.9 fusion.40
  41.6 0.0 copy-done.1
  41.7 0.0 copy-done.2
  41.7 3.0 %bitcast_add_fusion = f32[1024,896]{0,1:T(8,128)} fusion(f32[1024,384]{0,1:T(8,128)S(1)} %fusion.40, bf16[1024,384]{1,0:T(8,128)(2,1)S(1)} %all_gather.6, bf16[384,512]{1,0:T(8,128)(2,1)S(1)} %copy-done.1, bf16[384,384]{1,0:T(8,128)(2,1)S(1)} %copy-done.2), kind=kOutput, calls=%fused_computation.2 | convolution fusion | flops 706936832 | bytes 6717440 | tf_op jit(solution)/shard_map/dot_general | solution.py:112
  44.6 0.0 reduce-scatter.2.cloned.1.call-update
  44.7 0.0 all-gather.2.cloned.1.call-start
  44.7 46.8 %reduce-scatter.2.cloned.1.call-done = f32[256,896]{0,1:T(8,128)} async-done(((f32[1024,896]{0,1:T(8,128)}), f32[256,896]{0,1:T(8,128)}) %reduce-scatter.2.cloned.1.call-update) | async-done | bytes 917520 | tf_op jit(solution)/shard_map/reduce_scatter | solution.py:113
  91.6 1.2 convert.4
  92.8 0.7 slice.33
  93.5 0.0 all-gather.2.cloned.1.call-update
  93.6 0.1 dynamic_slice.16
  93.7 0.8 fusion.10
  94.5 1.8 %copy.26 = bf16[256,512]{1,0:T(8,128)(2,1)} copy(bf16[256,512]{0,1:T(8,128)(2,1)} %slice.33) | data formatting | bytes 524288
  96.3 25.1 %all-gather.2.cloned.1.call-done = bf16[1024,512]{0,1:T(8,128)(2,1)} async-done(((bf16[256,512]{0,1:T(8,128)(2,1)}), bf16[1024,512]{0,1:T(8,128)(2,1)}) %all-gather.2.cloned.1.call-update) | async-done | bytes 1048592 | tf_op jit(solution)/shard_map/all_gather | solution.py:127
  121.4 1.7 %fusion = (f32[3,256]{1,0:T(4,128)S(1)}, f32[1024,256,3]{1,0,2:T(8,128)S(1)}) fusion(pred[256,1024]{0,1:T(8,128)(4,1)S(1)} %fusion.10, bf16[256,3,128]{0,2,1:T(8,128)(2,1)S(1)} %bitcast.66, bf16[1024,512]{0,1:T(8,128)(2,1)} %all-gather.2.cloned.1.call-done, s32[]{:T(128)S(6)} %select_n.122), kind=kOutput, calls=%fused_computation.5 | convolution fusion | flops 203685120 | bytes 3869700 | tf_op jit(solution)/shard_map/qhd,kd->hqk/dot_general | solution.py:50
  123.1 0.8 fusion.1
  123.9 1.9 %fusion.14 = bf16[256,3,128]{0,2,1:T(8,128)(2,1)S(1)} fusion(f32[1024,256,3]{1,0,2:T(8,128)S(1)} %get-tuple-element.21, f32[3,256]{1,0:T(4,128)S(1)} %broadcast_maximum_fusion, pred[256,1024]{0,1:T(8,128)(4,1)S(1)} %fusion.10, bf16[1024,512]{0,1:T(8,128)(2,1)} %all-gather.2.cloned.1.call-done, s32[]{:T(128)S(6)} %select_n.125, f32[256,3]{0,1:T(4,128)S(1)} %bitcast.71), kind=kOutput, calls=%fused_computation.16 | convolution fusion | flops 205455360 | bytes 3872772 | tf_op jit(solution)/shard_map/hqk,kd->hqd/dot_general | solution.py:57
  125.8 0.8 copy.25
  (13 shorter events, 0.2 us)
Async XLA Ops:
  7.2 1.2 copy-start
  7.2 11.3 %copy-start.4 = (s32[16,8]{0,1:T(8,128)S(1)}, s32[16,8]{0,1:T(8,128)}, u32[]{:S(2)}) copy-start(s32[16,8]{0,1:T(8,128)} %param.13) | copy-start | bytes 1540
  7.2 11.3 %copy-start.5 = (s32[16,8]{0,1:T(8,128)S(1)}, s32[16,8]{0,1:T(8,128)}, u32[]{:S(2)}) copy-start(s32[16,8]{0,1:T(8,128)} %param.12) | copy-start | bytes 1540
  7.2 18.8 %copy-start.3 = (bf16[256,384]{1,0:T(8,128)(2,1)S(1)}, bf16[256,384]{1,0:T(8,128)(2,1)}, u32[]{:S(2)}) copy-start(bf16[256,384]{1,0:T(8,128)(2,1)} %param.7) | copy-start | bytes 589828
  11.6 28.6 %all-to-all-start = ((bf16[16,32,384]{2,1,0:T(8,128)(2,1)}), bf16[16,32,384]{2,1,0:T(8,128)(2,1)S(1)}, u32[]{:S(2)}, u32[]{:S(2)}) async-start(bf16[16,32,384]{2,1,0:T(8,128)(2,1)} %pad_maximum_fusion), calls=%async_computation | async-start | bytes 786432 | tf_op jit(solution)/shard_map/all_to_all | solution.py:102
  18.4 73.2 %reduce-scatter.2.cloned.1.call-start = ((), (), s32[]{:S(2)}) async-start(), calls=%async_computation.2 | async-start | bytes 4587520 | tf_op jit(solution)/shard_map/reduce_scatter | solution.py:113
  26.1 15.6 %copy-start.1 = (bf16[384,512]{1,0:T(8,128)(2,1)S(1)}, bf16[384,512]{1,0:T(8,128)(2,1)}, u32[]{:S(2)}) copy-start(bf16[384,512]{1,0:T(8,128)(2,1)} %param.9) | copy-start | bytes 1179652
  26.1 15.6 %copy-start.2 = (bf16[384,384]{1,0:T(8,128)(2,1)S(1)}, bf16[384,384]{1,0:T(8,128)(2,1)}, u32[]{:S(2)}) copy-start(bf16[384,384]{1,0:T(8,128)(2,1)} %param.8) | copy-start | bytes 884740
  44.7 76.7 %all-gather.2.cloned.1.call-start = ((), (), s32[]{:S(2)}) async-start(), calls=%async_computation.3 | async-start | bytes 1310720 | tf_op jit(solution)/shard_map/all_gather | solution.py:127
Sparse Core Ops, SparseCore 0:
  44.8 46.7 reduce-scatter.1
  93.7 27.6 all-gather.1

commit v2 on v1

--- a/solution.py
+++ b/solution.py
@@ -108,12 +108,14 @@
     kept_cols = rank_owner[None, :] == token_holder[:, None]
     reduced = jnp.where(kept_cols, reduced, 0.0)
     adapter_term = jnp.dot(reduced, flat_up, precision=lax.Precision.HIGHEST)
-    both_weights = jnp.concatenate([w_query, w_key_value], axis=1)
+    kv_share = kv_cols // lax.axis_size("row")
+    kv_slice = lax.dynamic_slice_in_dim(w_key_value, row_index * kv_share, kv_share, 1)
+    both_weights = jnp.concatenate([w_query, kv_slice], axis=1)
     partial_value = jnp.dot(gathered, both_weights, preferred_element_type=jnp.float32)
     summed = lax.psum_scatter(
         partial_value
         + jnp.concatenate(
-            [adapter_term, jnp.zeros((own_rows * lax.axis_size("col"), kv_cols), jnp.float32)],
+            [adapter_term, jnp.zeros((own_rows * lax.axis_size("col"), kv_share), jnp.float32)],
             axis=1,
         ),
         "col",
@@ -121,10 +123,17 @@
         tiled=True,
     )
     query_rows = summed[:, :query_cols].astype(jnp.bfloat16)
-    kv_cache = summed[:, query_cols:].astype(jnp.bfloat16)
-    attend, initial = make_attend(query_rows, segment, first_row, kv_group, head_size, kv_half)
+    kv_cache = lax.all_gather(summed[:, query_cols:].astype(jnp.bfloat16), "row", axis=1, tiled=True)
+    head_kv = jnp.concatenate(
+        [
+            lax.dynamic_slice_in_dim(kv_cache, kv_group * head_size, head_size, 1),
+            lax.dynamic_slice_in_dim(kv_cache, kv_half + kv_group * head_size, head_size, 1),
+        ],
+        axis=1,
+    )
+    attend, initial = make_attend(query_rows, segment, first_row, 0, head_size, head_size)
     running_max, running_sum, running_out = attend(
-        initial, lax.all_gather(kv_cache, "col", axis=0, tiled=True), jnp.int32(0)
+        initial, lax.all_gather(head_kv, "col", axis=0, tiled=True), jnp.int32(0)
     )
     attention = (running_out / running_sum[:, :, None]).astype(jnp.bfloat16)
     attention = jnp.transpose(attention, (1, 0, 2)).reshape(own_rows, query_cols)

time: 136 us -> 118 us (0.87)
  waiting for transfers between devices: 71.9 us -> 33.1 us
  blocking collectives: 14.2 us -> 39.5 us
  matrix products: 7.95 us -> 5.22 us
    all_gather x0 -> x2, blocking collectives: none -> 25.4 us  [the longest x1 12.8 us: body(): lax.all_gather(head_kv, 'col', axis=0, tiled=True)]
    all_gather x1 -> x0, waiting for transfers between devices: 25.1 us -> none  [body(): lax.all_gather(kv_cache, 'col', axis=0, tiled=True)]
    reduce_scatter x1, waiting for transfers between devices: 46.8 us -> 33.1 us  [body(): lax.psum_scatter(partial_value + jnp.concatenate([adapter_term, jnp.zeros...]
    unnamed x14 -> x12, local copies, waits for them, and re-layouts: 2.93 us -> 1.97 us
  transfers between devices with their start and end apart: 3 -> 2, of which waited for: 2 -> 1; matrix products, arithmetic and copies ran while one was open for 7% -> 7% of each run, Pallas kernels for 0% -> 0%
where the time goes in v2:
time: 118 us; the launch traced here: 116 us
  blocking collectives  39.5 us (33%)
  waiting for transfers between devices  33.1 us (28%)
  between operations  15 us (13%)
  other arithmetic  10.7 us (9%)
  starting transfers between devices  6.81 us (6%)
  local copies, waits for them, and re-layouts  6.03 us (5%)
  matrix products  5.22 us (4%)
    reduce_scatter x1, waiting for transfers between devices, body(): lax.psum_scatter(partial_value + jnp.concatenate([adapter_term, jnp.zeros...  33.1 us
    all_gather x1, blocking collectives, body(): gathered = lax.all_gather(hidden_states, 'row', axis=0, tiled=True)  14.2 us
    all_gather x1, blocking collectives, body(): lax.all_gather(head_kv, 'col', axis=0, tiled=True)  12.8 us
    all_gather x1, blocking collectives, body(): lax.all_gather(summed[:, query_cols:].astype(jnp.bfloat16), 'row', axis=1...  12.6 us
    all_to_all x1, starting transfers between devices, body(): lax.all_to_all(outgoing, 'dp', split_axis=0, concat_axis=0, tiled=True)  6.77 us
    gather x2, other arithmetic, body(): token_holder = jnp.where(in_request, holders[request_of], -1)  4.55 us
  transfers between devices with their start and end apart: 2, of which 1 were waited for; matrix products, arithmetic and copies ran while one was open for 7% of the time, Pallas kernels for 0%

profile of v2, /device:TPU:160, one launch (start us, length us, event | category | flops | bytes accessed | tf_op | source)
XLA Modules:
  0.0 116.4 jit_solution(375800416341270315)
XLA Ops:
  7.2 0.0 copy-start
  7.2 0.0 copy-start.3
  7.2 0.0 copy-start.4
  7.2 0.0 copy-start.2
  7.2 0.8 fusion.23
  8.0 0.3 copy-done
  8.3 0.6 gather_fusion.1
  8.9 1.7 %gather_fusion = bf16[16,384,16]{1,2,0:T(8,128)(2,1)S(1)} fusion(bf16[64,384,16]{1,2,0:T(8,128)(2,1)} %param.10, s32[1024]{0:T(1024)S(1)} %pad_clamp_fusion), kind=kCustom, calls=%fused_computation | custom fusion | bytes 393280 | tf_op jit(solution)/shard_map/jit(_take)/gather | solution.py:99
  10.6 0.1 broadcast_select_fusion
  10.7 0.1 select_bitcast_fusion
  10.9 0.8 pad_maximum_fusion
  11.6 6.8 %all-to-all-start = ((bf16[16,32,384]{2,1,0:T(8,128)(2,1)}), bf16[16,32,384]{2,1,0:T(8,128)(2,1)S(1)}, u32[]{:S(2)}, u32[]{:S(2)}) async-start(bf16[16,32,384]{2,1,0:T(8,128)(2,1)} %pad_maximum_fusion), calls=%async_computation | async-start | bytes 786432 | tf_op jit(solution)/shard_map/all_to_all | solution.py:102
  18.4 0.0 reduce-scatter.2.cloned.1.call-start
  18.5 0.0 copy-done.3
  18.5 0.0 copy-done.4
  18.5 0.7 fusion.31
  19.9 0.1 subtract_reduce_fusion
  20.0 0.1 convert_reduce_fusion
  20.1 0.7 fusion.33
  20.9 0.9 constant_dynamic-slice_fusion.2
  21.8 4.5 %compare_select_fusion.1 = s32[1024,1]{0,1:T(1,128)S(1)} fusion(s32[]{:T(128)} %bitcast.3, s32[]{:T(128)} %bitcast.4, s32[]{:T(128)} %bitcast.5, s32[]{:T(128)} %bitcast.6, s32[]{:T(128)} %bitcast.7, s32[]{:T(128)} %bitcast.9, s32[]{:T(128)} %bitcast.8, s32[1024,1]{0,1:T(1,128)S(1)} %bitcast.69), kind=kLoop, calls=%fused_computation.31 | loop fusion | flops 15360 | bytes 8220 | tf_op jit(solution)/shard_map/gather | solution.py:107
  26.3 0.7 select_select_fusion
  26.9 0.0 copy-done.2
  27.0 0.0 copy-start.1
  27.0 14.2 %all_gather.9 = bf16[1024,384]{1,0:T(8,128)(2,1)S(1)} all-gather(bf16[256,384]{1,0:T(8,128)(2,1)S(1)} %copy-done.2), channel_id=1, replica_groups=mesh['row'=4,'col'=4,'dp'=16] {'row'}, dimensions={0}, use_global_device_ids=true | all-gather | bytes 983040 | tf_op jit(solution)/shard_map/all_gather | solution.py:75
  41.1 0.0 all-to-all-done
  41.2 0.5 fusion.6
  41.7 0.9 fusion.34
  42.5 0.0 copy-done.1
  42.6 2.1 %bitcast_add_fusion = f32[1024,512]{0,1:T(8,128)} fusion(f32[1024,384]{0,1:T(8,128)S(1)} %fusion.34, bf16[1024,384]{1,0:T(8,128)(2,1)S(1)} %all_gather.9, bf16[384,128]{1,0:T(8,128)(2,1)S(1)} %constant_dynamic-slice_fusion.2, bf16[384,384]{1,0:T(8,128)(2,1)S(1)} %copy-done.1), kind=kOutput, calls=%fused_computation.7 | convolution fusion | flops 403963904 | bytes 4849664 | tf_op jit(solution)/shard_map/dot_general | solution.py:114
  44.7 0.0 reduce-scatter.2.cloned.1.call-update
  44.7 0.1 dynamic_slice.25
  44.8 0.8 fusion.10
  45.6 33.1 %reduce-scatter.2.cloned.1.call-done = f32[256,512]{0,1:T(8,128)} async-done(((f32[1024,512]{0,1:T(8,128)}), f32[256,512]{0,1:T(8,128)}) %reduce-scatter.2.cloned.1.call-update) | async-done | bytes 524304 | tf_op jit(solution)/shard_map/reduce_scatter | solution.py:115
  78.7 1.1 convert.4
  79.9 12.6 %all_gather.10 = bf16[256,512]{0,1:T(8,128)(2,1)S(1)} all-gather(bf16[256,128]{0,1:T(8,128)(2,1)S(1)} %slice.33), channel_id=1, replica_groups=mesh['row'=4,'col'=4,'dp'=16] {'row'}, dimensions={1}, use_global_device_ids=true | all-gather | bytes 327680 | tf_op jit(solution)/shard_map/all_gather | solution.py:126
  92.4 0.8 copy.26
  93.3 12.8 %all_gather.11 = bf16[1024,256]{0,1:T(8,128)(2,1)S(1)} all-gather(bf16[256,256]{0,1:T(8,128)(2,1)S(1)} %pad_maximum_fusion.1), channel_id=1, replica_groups=mesh['row'=4,'col'=4,'dp'=16] {'col'}, dimensions={0}, use_global_device_ids=true | all-gather | bytes 655360 | tf_op jit(solution)/shard_map/all_gather | solution.py:136
  106.1 0.8 fusion
  106.9 0.8 fusion.1
  107.7 1.0 fusion.14
  108.7 0.8 copy.25
  (16 shorter events, 0.2 us)
Async XLA Ops:
  7.2 1.2 copy-start
  7.2 11.3 %copy-start.3 = (s32[16,8]{0,1:T(8,128)S(1)}, s32[16,8]{0,1:T(8,128)}, u32[]{:S(2)}) copy-start(s32[16,8]{0,1:T(8,128)} %param.13) | copy-start | bytes 1540
  7.2 11.3 %copy-start.4 = (s32[16,8]{0,1:T(8,128)S(1)}, s32[16,8]{0,1:T(8,128)}, u32[]{:S(2)}) copy-start(s32[16,8]{0,1:T(8,128)} %param.12) | copy-start | bytes 1540
  7.2 19.8 %copy-start.2 = (bf16[256,384]{1,0:T(8,128)(2,1)S(1)}, bf16[256,384]{1,0:T(8,128)(2,1)}, u32[]{:S(2)}) copy-start(bf16[256,384]{1,0:T(8,128)(2,1)} %param.7) | copy-start | bytes 589828
  11.6 29.5 %all-to-all-start = ((bf16[16,32,384]{2,1,0:T(8,128)(2,1)}), bf16[16,32,384]{2,1,0:T(8,128)(2,1)S(1)}, u32[]{:S(2)}, u32[]{:S(2)}) async-start(bf16[16,32,384]{2,1,0:T(8,128)(2,1)} %pad_maximum_fusion), calls=%async_computation | async-start | bytes 786432 | tf_op jit(solution)/shard_map/all_to_all | solution.py:102
  18.4 60.3 %reduce-scatter.2.cloned.1.call-start = ((), (), s32[]{:S(2)}) async-start(), calls=%async_computation.2 | async-start | bytes 2621440 | tf_op jit(solution)/shard_map/reduce_scatter | solution.py:115
  27.0 15.6 %copy-start.1 = (bf16[384,384]{1,0:T(8,128)(2,1)S(1)}, bf16[384,384]{1,0:T(8,128)(2,1)}, u32[]{:S(2)}) copy-start(bf16[384,384]{1,0:T(8,128)(2,1)} %param.8) | copy-start | bytes 884740
Sparse Core Ops, SparseCore 0:
  44.8 33.8 reduce-scatter.1

commit v3 on v2

--- a/solution.py
+++ b/solution.py
@@ -104,7 +104,10 @@
     flat_up = incoming[:, rank_size:, :].reshape(dp_size * rank_size, query_cols).astype(jnp.float32)
     rank_owner = jnp.arange(dp_size * rank_size, dtype=jnp.int32) // rank_size
     reduced = jnp.dot(gathered, flat_down, preferred_element_type=jnp.float32)
-    token_holder = jnp.where(in_request, holders[request_of], -1)
+    request_ids = jnp.arange(requests, dtype=jnp.int32)
+    token_holder = jnp.sum(
+        jnp.where(segment[:, None] == request_ids[None, :] + 1, holders[None, :] + 1, 0), axis=1
+    ) - 1
     kept_cols = rank_owner[None, :] == token_holder[:, None]
     reduced = jnp.where(kept_cols, reduced, 0.0)
     adapter_term = jnp.dot(reduced, flat_up, precision=lax.Precision.HIGHEST)
@@ -123,17 +126,20 @@
         tiled=True,
     )
     query_rows = summed[:, :query_cols].astype(jnp.bfloat16)
-    kv_cache = lax.all_gather(summed[:, query_cols:].astype(jnp.bfloat16), "row", axis=1, tiled=True)
-    head_kv = jnp.concatenate(
-        [
-            lax.dynamic_slice_in_dim(kv_cache, kv_group * head_size, head_size, 1),
-            lax.dynamic_slice_in_dim(kv_cache, kv_half + kv_group * head_size, head_size, 1),
-        ],
-        axis=1,
+    kv_pieces = lax.all_gather(summed[:, query_cols:].astype(jnp.bfloat16), ("row", "col"), axis=0)
+    kv_pieces = kv_pieces.reshape(lax.axis_size("row"), lax.axis_size("col"), own_rows, kv_share)
+    own_pieces = lax.dynamic_index_in_dim(kv_pieces, col_index, 1, keepdims=False)
+    kv_cache = jnp.transpose(own_pieces, (1, 0, 2)).reshape(own_rows, kv_cols)
+    parts_per_head = head_size // kv_share
+    key_all = lax.dynamic_slice_in_dim(kv_pieces, kv_group * parts_per_head, parts_per_head, 0)
+    value_all = lax.dynamic_slice_in_dim(
+        kv_pieces, (kv_heads + kv_group) * parts_per_head, parts_per_head, 0
     )
+    key_all = jnp.transpose(key_all, (1, 2, 0, 3)).reshape(block_len, head_size)
+    value_all = jnp.transpose(value_all, (1, 2, 0, 3)).reshape(block_len, head_size)
     attend, initial = make_attend(query_rows, segment, first_row, 0, head_size, head_size)
     running_max, running_sum, running_out = attend(
-        initial, lax.all_gather(head_kv, "col", axis=0, tiled=True), jnp.int32(0)
+        initial, jnp.concatenate([key_all, value_all], axis=1), jnp.int32(0)
     )
     attention = (running_out / running_sum[:, :, None]).astype(jnp.bfloat16)
     attention = jnp.transpose(attention, (1, 0, 2)).reshape(own_rows, query_cols)

time: 118 us -> 140 us (1.19)
  waiting for transfers between devices: 33.1 us -> 82.1 us
  blocking collectives: 39.5 us -> 14.2 us
  other arithmetic: 10.7 us -> 5.54 us
  local copies, waits for them, and re-layouts: 6.03 us -> 9.01 us
    all_gather x0 -> x1, waiting for transfers between devices: none -> 48.2 us  [body(): lax.all_gather(summed[:, query_cols:].astype(jnp.bfloat16), ('row', 'col'...]
    all_gather x2 -> x0, blocking collectives: 25.4 us -> none  [the longest x1 12.8 us: body(): lax.all_gather(head_kv, 'col', axis=0, tiled=True)]
    gather x2 -> x0, other arithmetic: 4.55 us -> none  [body(): token_holder = jnp.where(in_request, holders[request_of], -1)]
    reshape x0 -> x1, local copies, waits for them, and re-layouts: none -> 1.85 us  [body(): kv_pieces.reshape(lax.axis_size('row'), lax.axis_size('col'), own_rows, k...]
  transfers between devices with their start and end apart: 2 -> 3, of which waited for: 1 -> 2; matrix products, arithmetic and copies ran while one was open for 7% -> 2% of each run, Pallas kernels for 0% -> 0%
where the time goes in v3:
time: 140 us; the launch traced here: 138 us
  waiting for transfers between devices  82.1 us (59%)
  between operations  15 us (11%)
  blocking collectives  14.2 us (10%)
  local copies, waits for them, and re-layouts  9.01 us (6%)
  starting transfers between devices  6.85 us (5%)
  other arithmetic  5.54 us (4%)
  matrix products  5.16 us (4%)
    all_gather x1, waiting for transfers between devices, body(): lax.all_gather(summed[:, query_cols:].astype(jnp.bfloat16), ('row', 'col'...  48.2 us
    reduce_scatter x1, waiting for transfers between devices, body(): lax.psum_scatter(partial_value + jnp.concatenate([adapter_term, jnp.zeros...  33.8 us
    all_gather x1, blocking collectives, body(): gathered = lax.all_gather(hidden_states, 'row', axis=0, tiled=True)  14.2 us
    all_to_all x1, starting transfers between devices, body(): lax.all_to_all(outgoing, 'dp', split_axis=0, concat_axis=0, tiled=True)  6.77 us
  transfers between devices with their start and end apart: 3, of which 2 were waited for; matrix products, arithmetic and copies ran while one was open for 2% of the time, Pallas kernels for 0%

profile of v3, /device:TPU:160, one launch (start us, length us, event | category | flops | bytes accessed | tf_op | source)
XLA Modules:
  0.0 137.8 jit_solution(9572171960682573029)
XLA Ops:
  7.2 0.0 copy-start
  7.2 0.0 copy-start.3
  7.2 0.0 copy-start.4
  7.2 0.0 copy-start.2
  7.2 0.8 fusion.25
  8.0 0.3 copy-done
  8.3 0.6 gather_fusion.1
  8.9 1.7 %gather_fusion = bf16[16,384,16]{1,2,0:T(8,128)(2,1)S(1)} fusion(bf16[64,384,16]{1,2,0:T(8,128)(2,1)} %param.10, s32[1024]{0:T(1024)S(1)} %pad_clamp_fusion), kind=kCustom, calls=%fused_computation | custom fusion | bytes 393280 | tf_op jit(solution)/shard_map/jit(_take)/gather | solution.py:99
  10.6 0.1 broadcast_select_fusion
  10.7 0.1 select_bitcast_fusion
  10.9 0.8 pad_maximum_fusion
  11.6 6.8 %all-to-all-start = ((bf16[16,32,384]{2,1,0:T(8,128)(2,1)}), bf16[16,32,384]{2,1,0:T(8,128)(2,1)S(1)}, u32[]{:S(2)}, u32[]{:S(2)}) async-start(bf16[16,32,384]{2,1,0:T(8,128)(2,1)} %pad_maximum_fusion), calls=%async_computation | async-start | bytes 786432 | tf_op jit(solution)/shard_map/all_to_all | solution.py:102
  18.4 0.0 reduce-scatter.2.cloned.1.call-start
  18.5 0.0 copy-done.3
  18.5 0.0 copy-done.4
  18.5 0.7 fusion.34
  19.9 0.1 subtract_reduce_fusion
  20.0 0.1 convert_reduce_fusion
  20.1 0.9 constant_dynamic-slice_fusion.3
  21.0 0.1 select_reduce_fusion
  21.1 0.0 copy-done.2
  21.1 0.0 copy-start.1
  21.1 14.2 %all_gather.9 = bf16[1024,384]{1,0:T(8,128)(2,1)S(1)} all-gather(bf16[256,384]{1,0:T(8,128)(2,1)S(1)} %copy-done.2), channel_id=1, replica_groups=mesh['row'=4,'col'=4,'dp'=16] {'row'}, dimensions={0}, use_global_device_ids=true | all-gather | bytes 983040 | tf_op jit(solution)/shard_map/all_gather | solution.py:75
  35.3 0.0 all-to-all-done
  35.3 0.5 fusion.6
  35.8 0.9 fusion.36
  36.7 0.0 copy-done.1
  36.7 2.1 %bitcast_add_fusion = f32[1024,512]{0,1:T(8,128)} fusion(f32[1024,384]{0,1:T(8,128)S(1)} %fusion.36, bf16[1024,384]{1,0:T(8,128)(2,1)S(1)} %all_gather.9, bf16[384,128]{1,0:T(8,128)(2,1)S(1)} %constant_dynamic-slice_fusion.3, bf16[384,384]{1,0:T(8,128)(2,1)S(1)} %copy-done.1), kind=kOutput, calls=%fused_computation.7 | convolution fusion | flops 403963904 | bytes 4849664 | tf_op jit(solution)/shard_map/dot_general | solution.py:117
  38.8 0.0 reduce-scatter.2.cloned.1.call-update
  38.9 0.0 all-gather.3.cloned.1.call-start
  38.9 33.8 %reduce-scatter.2.cloned.1.call-done = f32[256,512]{0,1:T(8,128)} async-done(((f32[1024,512]{0,1:T(8,128)}), f32[256,512]{0,1:T(8,128)}) %reduce-scatter.2.cloned.1.call-update) | async-done | bytes 524304 | tf_op jit(solution)/shard_map/reduce_scatter | solution.py:118
  72.7 1.1 convert.4
  73.8 0.6 slice.24
  74.4 0.0 all-gather.3.cloned.1.call-update
  74.5 0.1 dynamic_slice.23
  74.6 0.8 fusion.10
  75.4 48.2 %all-gather.3.cloned.1.call-done = bf16[4096,128]{0,1:T(8,128)(2,1)} async-done(((bf16[256,128]{0,1:T(8,128)(2,1)}), bf16[4096,128]{0,1:T(8,128)(2,1)}) %all-gather.3.cloned.1.call-update) | async-done | bytes 1048592 | tf_op jit(solution)/shard_map/all_gather | solution.py:129
  123.6 1.8 %reshape.151 = bf16[4,4,256,128]{2,1,0,3:T(4,128)(2,1)S(1)} reshape(bf16[4096,128]{0,1:T(8,128)(2,1)} %all-gather.3.cloned.1.call-done) | data formatting | bytes 2097152 | tf_op jit(solution)/shard_map/reshape | solution.py:130
  125.5 0.5 constant_dynamic-slice_fusion.2
  126.1 0.1 copy.40
  126.1 0.8 copy.35
  127.0 0.2 constant_dynamic-slice_fusion.1
  127.2 0.2 copy.29
  127.4 0.2 reshape.174
  127.6 0.7 fusion
  128.3 0.8 fusion.1
  129.1 1.0 fusion.14
  130.1 0.8 copy.34
  (12 shorter events, 0.1 us)
Async XLA Ops:
  7.2 1.2 copy-start
  7.2 11.3 %copy-start.3 = (s32[16,8]{0,1:T(8,128)S(1)}, s32[16,8]{0,1:T(8,128)}, u32[]{:S(2)}) copy-start(s32[16,8]{0,1:T(8,128)} %param.13) | copy-start | bytes 1540
  7.2 11.3 %copy-start.4 = (s32[16,8]{0,1:T(8,128)S(1)}, s32[16,8]{0,1:T(8,128)}, u32[]{:S(2)}) copy-start(s32[16,8]{0,1:T(8,128)} %param.12) | copy-start | bytes 1540
  7.2 13.9 %copy-start.2 = (bf16[256,384]{1,0:T(8,128)(2,1)S(1)}, bf16[256,384]{1,0:T(8,128)(2,1)}, u32[]{:S(2)}) copy-start(bf16[256,384]{1,0:T(8,128)(2,1)} %param.7) | copy-start | bytes 589828
  11.6 23.7 %all-to-all-start = ((bf16[16,32,384]{2,1,0:T(8,128)(2,1)}), bf16[16,32,384]{2,1,0:T(8,128)(2,1)S(1)}, u32[]{:S(2)}, u32[]{:S(2)}) async-start(bf16[16,32,384]{2,1,0:T(8,128)(2,1)} %pad_maximum_fusion), calls=%async_computation | async-start | bytes 786432 | tf_op jit(solution)/shard_map/all_to_all | solution.py:102
  18.4 54.3 %reduce-scatter.2.cloned.1.call-start = ((), (), s32[]{:S(2)}) async-start(), calls=%async_computation.2 | async-start | bytes 2621440 | tf_op jit(solution)/shard_map/reduce_scatter | solution.py:118
  21.1 15.6 %copy-start.1 = (bf16[384,384]{1,0:T(8,128)(2,1)S(1)}, bf16[384,384]{1,0:T(8,128)(2,1)}, u32[]{:S(2)}) copy-start(bf16[384,384]{1,0:T(8,128)(2,1)} %param.8) | copy-start | bytes 884740
  38.9 84.8 %all-gather.3.cloned.1.call-start = ((), (), s32[]{:S(2)}) async-start(), calls=%async_computation.3 | async-start | bytes 1114112 | tf_op jit(solution)/shard_map/all_gather | solution.py:129
Sparse Core Ops, SparseCore 0:
  39.0 33.6 reduce-scatter.1
  75.7 47.9 all-gather.2

commit v4 on v2

--- a/solution.py
+++ b/solution.py
@@ -67,12 +67,45 @@
     return (attend, initial)
 
 
+def shifted_copies(x, axis_name):
+    size = lax.axis_size(axis_name)
+    copies = [x]
+    for shift in range(1, size):
+        perm = [(i, (i - shift) % size) for i in range(size)]
+        copies.append(lax.ppermute(x, axis_name, perm))
+    return copies
+
+
+def ring_gather(x, axis_name, axis):
+    size = lax.axis_size(axis_name)
+    me = lax.axis_index(axis_name)
+    copies = shifted_copies(x, axis_name)
+    doubled = jnp.stack(copies + copies, axis=0)
+    ordered = lax.dynamic_slice_in_dim(doubled, size - me, size, 0)
+    moved = jnp.moveaxis(ordered, 0, axis)
+    shape = list(x.shape)
+    shape[axis] = shape[axis] * size
+    return moved.reshape(shape)
+
+
+def ring_reduce_scatter(x, axis_name):
+    size = lax.axis_size(axis_name)
+    me = lax.axis_index(axis_name)
+    chunk = x.shape[0] // size
+    total = lax.dynamic_slice_in_dim(x, me * chunk, chunk, 0)
+    for shift in range(1, size):
+        perm = [(i, (i + shift) % size) for i in range(size)]
+        piece = lax.dynamic_slice_in_dim(x, ((me + shift) % size) * chunk, chunk, 0)
+        total = total + lax.ppermute(piece, axis_name, perm)
+    return total
+
+
 def body(hidden_states, w_query, w_key_value, adapter_down, adapter_up, req_lengths, req_adapter):
     dp_size = lax.axis_size("dp")
     block_index = lax.axis_index("dp")
     col_index = lax.axis_index("col")
     row_index = lax.axis_index("row")
-    gathered = lax.all_gather(hidden_states, "row", axis=0, tiled=True)
+    gathered = ring_gather(hidden_states, "row", 0)
     block_len = gathered.shape[0]
     query_cols = w_query.shape[1]
     kv_cols = w_key_value.shape[1]
@@ -104,7 +137,10 @@
     flat_up = incoming[:, rank_size:, :].reshape(dp_size * rank_size, query_cols).astype(jnp.float32)
     rank_owner = jnp.arange(dp_size * rank_size, dtype=jnp.int32) // rank_size
     reduced = jnp.dot(gathered, flat_down, preferred_element_type=jnp.float32)
-    token_holder = jnp.where(in_request, holders[request_of], -1)
+    request_ids = jnp.arange(requests, dtype=jnp.int32)
+    token_holder = jnp.sum(
+        jnp.where(segment[:, None] == request_ids[None, :] + 1, holders[None, :] + 1, 0), axis=1
+    ) - 1
     kept_cols = rank_owner[None, :] == token_holder[:, None]
     reduced = jnp.where(kept_cols, reduced, 0.0)
     adapter_term = jnp.dot(reduced, flat_up, precision=lax.Precision.HIGHEST)
@@ -112,18 +148,16 @@
     kv_slice = lax.dynamic_slice_in_dim(w_key_value, row_index * kv_share, kv_share, 1)
     both_weights = jnp.concatenate([w_query, kv_slice], axis=1)
     partial_value = jnp.dot(gathered, both_weights, preferred_element_type=jnp.float32)
-    summed = lax.psum_scatter(
+    summed = ring_reduce_scatter(
         partial_value
         + jnp.concatenate(
             [adapter_term, jnp.zeros((own_rows * lax.axis_size("col"), kv_share), jnp.float32)],
             axis=1,
         ),
         "col",
-        scatter_dimension=0,
-        tiled=True,
     )
     query_rows = summed[:, :query_cols].astype(jnp.bfloat16)
-    kv_cache = lax.all_gather(summed[:, query_cols:].astype(jnp.bfloat16), "row", axis=1, tiled=True)
+    kv_cache = ring_gather(summed[:, query_cols:].astype(jnp.bfloat16), "row", 1)
     head_kv = jnp.concatenate(
         [
             lax.dynamic_slice_in_dim(kv_cache, kv_group * head_size, head_size, 1),
@@ -133,7 +167,7 @@
     )
     attend, initial = make_attend(query_rows, segment, first_row, 0, head_size, head_size)
     running_max, running_sum, running_out = attend(
-        initial, lax.all_gather(head_kv, "col", axis=0, tiled=True), jnp.int32(0)
+        initial, ring_gather(head_kv, "col", 0), jnp.int32(0)
     )
     attention = (running_out / running_sum[:, :, None]).astype(jnp.bfloat16)
     attention = jnp.transpose(attention, (1, 0, 2)).reshape(own_rows, query_cols)

time: 118 us -> 92.6 us (0.78)
  the two profiles are of different devices: /device:TPU:160 before, /device:TPU:1 now
where the time goes in v4:
time: 92.6 us; the launch traced here: 92.2 us
  waiting for transfers between devices  39 us (42%)
  starting transfers between devices  26.7 us (29%)
  local copies, waits for them, and re-layouts  14 us (15%)
  other arithmetic  5.91 us (6%)
  matrix products  4.89 us (5%)
  between operations  1.68 us (2%)
    ppermute x3, waiting for transfers between devices, ring_reduce_scatter(): total = total + lax.ppermute(piece, axis_name, perm)  22.4 us
    ppermute x9, starting transfers between devices, shifted_copies(): copies.append(lax.ppermute(x, axis_name, perm))  11.9 us
    ppermute x9, waiting for transfers between devices, shifted_copies(): copies.append(lax.ppermute(x, axis_name, perm))  11.6 us
    all_to_all x1, starting transfers between devices, body(): lax.all_to_all(outgoing, 'dp', split_axis=0, concat_axis=0, tiled=True)  9.99 us
    unnamed x35, local copies, waits for them, and re-layouts  6.65 us
    all_to_all x1, waiting for transfers between devices, body(): lax.all_to_all(outgoing, 'dp', split_axis=0, concat_axis=0, tiled=True)  5.02 us
    ppermute x3, starting transfers between devices, ring_reduce_scatter(): total = total + lax.ppermute(piece, axis_name, perm)  4.81 us
    dot_general x1, matrix products, body(): jnp.dot(gathered, both_weights, preferred_element_type=jnp.float32)  1.89 us
  transfers between devices with their start and end apart: 13, of which 8 were waited for; matrix products, arithmetic and copies ran while one was open for 16% of the time, Pallas kernels for 0%

profile of v4, /device:TPU:1, one launch (start us, length us, event | category | flops | bytes accessed | tf_op | source)
XLA Modules:
  0.0 92.2 jit_solution(10293217284336464306)
XLA Ops:
  0.6 0.0 copy-start
  0.6 3.6 %collective-permute-start = (bf16[256,384]{1,0:T(8,128)(2,1)}, bf16[256,384]{1,0:T(8,128)(2,1)S(1)}, u32[]{:S(2)}, u32[]{:S(2)}) collective-permute-start(bf16[256,384]{1,0:T(8,128)(2,1)} %param.7), channel_id=1, source_target_pairs={{0,192},{64,0},{128,64},{192,128},{1,193},{65,1},{129,65},{193,129... | collective-permute-start | bytes 589832 | tf_op jit(solution)/shard_map/ppermute | solution.py:75
  4.3 0.3 collective-permute-start.1
  4.6 0.7 collective-permute-start.2
  5.3 0.7 fusion.25
  6.1 0.6 gather_fusion.1
  6.7 0.0 copy-start.3
  6.7 1.8 %gather_fusion = bf16[16,384,16]{1,2,0:T(8,128)(2,1)S(1)} fusion(bf16[64,384,16]{1,2,0:T(8,128)(2,1)} %param.10, s32[1024]{0:T(1024)S(1)} %pad_clamp_fusion), kind=kCustom, calls=%fused_computation | custom fusion | bytes 393280 | tf_op jit(solution)/shard_map/jit(_take)/gather | solution.py:132
  8.4 0.0 copy-start.5
  8.5 0.0 copy-start.6
  8.5 0.1 broadcast_select_fusion
  8.6 0.1 select_bitcast_fusion
  8.7 0.8 pad_maximum_fusion
  9.5 10.0 %all-to-all-start = ((bf16[16,32,384]{2,1,0:T(8,128)(2,1)}), bf16[16,32,384]{2,1,0:T(8,128)(2,1)S(1)}, u32[]{:S(2)}, u32[]{:S(2)}) async-start(bf16[16,32,384]{2,1,0:T(8,128)(2,1)} %pad_maximum_fusion), calls=%async_computation | async-start | bytes 786432 | tf_op jit(solution)/shard_map/all_to_all | solution.py:135
  19.5 0.7 bitcast_dynamic-update-slice_fusion.6
  20.2 0.7 fusion.34
  21.6 0.1 subtract_reduce_fusion
  21.7 0.1 convert_reduce_fusion
  21.8 0.9 constant_dynamic-slice_fusion.7
  22.7 0.1 select_reduce_fusion
  22.8 0.0 collective-permute-done
  22.8 0.7 bitcast_dynamic-update-slice_fusion.4
  23.5 0.0 collective-permute-done.1
  23.5 0.7 bitcast_dynamic-update-slice_fusion.2
  24.2 0.0 collective-permute-done.2
  24.2 0.7 bitcast_dynamic-update-slice_fusion
  24.9 0.7 bitcast_dynamic-update-slice_fusion.7
  25.6 0.7 bitcast_dynamic-update-slice_fusion.5
  26.3 0.7 bitcast_dynamic-update-slice_fusion.3
  27.0 0.7 bitcast_dynamic-update-slice_fusion.1
  27.7 1.2 %constant_dynamic-slice_fusion.8 = bf16[4,256,384]{2,1,0:T(8,128)(2,1)S(1)} fusion(bf16[8,256,384]{2,1,0:T(8,128)(2,1)} %bitcast_dynamic-update-slice_fusion.1, s32[]{:T(128)S(6)} %select_n.129), kind=kLoop, calls=%fused_computation.84 | loop fusion | bytes 1572868 | tf_op jit(solution)/shard_map/dynamic_slice | solution.py:84
  28.9 5.0 %all-to-all-done = bf16[16,32,384]{2,1,0:T(8,128)(2,1)S(1)} async-done(((bf16[16,32,384]{2,1,0:T(8,128)(2,1)}), bf16[16,32,384]{2,1,0:T(8,128)(2,1)S(1)}, u32[]{:S(2)}, u32[]{:S(2)}) %all-to-all-start) | async-done | bytes 393248 | tf_op jit(solution)/shard_map/all_to_all | solution.py:135
  34.0 0.0 copy-start.4
  34.0 0.5 convolution_select_fusion
  34.5 0.9 fusion.36
  35.4 1.9 %pad_add_fusion = f32[1024,512]{0,1:T(8,128)S(1)} fusion(f32[1024,384]{0,1:T(8,128)S(1)} %fusion.36, bf16[1024,384]{1,0:T(8,128)(2,1)} %bitcast.90, bf16[384,128]{1,0:T(8,128)(2,1)S(1)} %constant_dynamic-slice_fusion.7, bf16[384,384]{1,0:T(8,128)(2,1)S(1)} %copy-done.4), kind=kOutput, calls=%fused_computation.7 | convolution fusion | flops 403963904 | bytes 4849664 | tf_op jit(solution)/shard_map/dot_general | solution.py:150
  37.3 1.2 %constant_dynamic-slice_fusion.6 = (f32[256,512]{0,1:T(8,128)}, f32[256,512]{0,1:T(8,128)S(1)}, f32[256,512]{0,1:T(8,128)}) fusion(f32[1024,512]{0,1:T(8,128)S(1)} %pad_add_fusion, s32[]{:T(128)S(6)} %select_n.144, s32[]{:T(128)S(6)} %select_n.148, s32[]{:T(128)S(6)} %select_n.146), kind=kLoop, calls=%fused_computation.82 | loop fusion | bytes 3145740 | tf_op jit(solution)/shard_map/dynamic_slice | solution.py:98
  38.4 1.2 %collective-permute-start.3 = (f32[256,512]{0,1:T(8,128)}, f32[256,512]{0,1:T(8,128)}, u32[]{:S(2)}, u32[]{:S(2)}) collective-permute-start(f32[256,512]{0,1:T(8,128)} %get-tuple-element.8), channel_id=1, source_target_pairs={{0,16},{16,32},{32,48},{48,0},{1,17},{17,33},{33,49},{49,1},{2,18}... | collective-permute-start | bytes 1572872 | tf_op jit(solution)/shard_map/ppermute | solution.py:99
  39.7 2.5 %collective-permute-start.4 = (f32[256,512]{0,1:T(8,128)}, f32[256,512]{0,1:T(8,128)}, u32[]{:S(2)}, u32[]{:S(2)}) collective-permute-start(f32[256,512]{0,1:T(8,128)} %get-tuple-element.10), channel_id=1, source_target_pairs={{0,32},{16,48},{32,0},{48,16},{1,33},{17,49},{33,1},{49,17},{2,34}... | collective-permute-start | bytes 1572872 | tf_op jit(solution)/shard_map/ppermute | solution.py:99
  42.1 1.1 %collective-permute-start.5 = (f32[256,512]{0,1:T(8,128)S(1)}, f32[256,512]{0,1:T(8,128)}, u32[]{:S(2)}, u32[]{:S(2)}) collective-permute-start(f32[256,512]{0,1:T(8,128)S(1)} %get-tuple-element.9), channel_id=1, source_target_pairs={{0,48},{16,0},{32,16},{48,32},{1,49},{17,1},{33,17},{49,33},{2,50}... | collective-permute-start | bytes 1572872 | tf_op jit(solution)/shard_map/ppermute | solution.py:99
  43.3 0.1 dynamic_slice.46
  43.3 10.0 %collective-permute-done.3 = f32[256,512]{0,1:T(8,128)} collective-permute-done((f32[256,512]{0,1:T(8,128)}, f32[256,512]{0,1:T(8,128)}, u32[]{:S(2)}, u32[]{:S(2)}) %collective-permute-start.3) | collective-permute-done | bytes 524320 | tf_op jit(solution)/shard_map/ppermute | solution.py:99
  53.3 12.2 %collective-permute-done.4 = f32[256,512]{0,1:T(8,128)} collective-permute-done((f32[256,512]{0,1:T(8,128)}, f32[256,512]{0,1:T(8,128)}, u32[]{:S(2)}, u32[]{:S(2)}) %collective-permute-start.4) | collective-permute-done | bytes 524320 | tf_op jit(solution)/shard_map/ppermute | solution.py:99
  65.5 0.2 collective-permute-done.5
  65.7 1.5 %add_convert_fusion = bf16[256,512]{0,1:T(8,128)(2,1)S(1)} fusion(f32[256,512]{0,1:T(8,128)} %collective-permute-done.5, f32[256,512]{0,1:T(8,128)} %collective-permute-done.4, f32[256,512]{0,1:T(8,128)} %collective-permute-done.3, f32[1024,512]{0,1:T(8,128)S(1)} %pad_add_fusion, s32[]{:T(128)S(6)} %select_n.128), kind=kLoop, calls=%fused_computation.16 | loop fusion | flops 524288 | bytes 2359300 | tf_op jit(solution)/shard_map/convert.1
  67.2 2.1 %collective-permute-start.6 = (bf16[256,128]{0,1:T(8,128)(2,1)S(1)}, bf16[256,128]{0,1:T(8,128)(2,1)S(1)}, u32[]{:S(2)}, u32[]{:S(2)}) collective-permute-start(bf16[256,128]{0,1:T(8,128)(2,1)S(1)} %slice.24), channel_id=1, source_target_pairs={{0,192},{64,0},{128,64},{192,128},{1,193},{65,1},{129,65},{193,129... | collective-permute-start | bytes 196616 | tf_op jit(solution)/shard_map/ppermute | solution.py:75
  69.3 1.4 %collective-permute-start.7 = (bf16[256,128]{0,1:T(8,128)(2,1)S(1)}, bf16[256,128]{0,1:T(8,128)(2,1)S(1)}, u32[]{:S(2)}, u32[]{:S(2)}) collective-permute-start(bf16[256,128]{0,1:T(8,128)(2,1)S(1)} %slice.24), channel_id=1, source_target_pairs={{0,128},{64,192},{128,0},{192,64},{1,129},{65,193},{129,1},{193,65... | collective-permute-start | bytes 196616 | tf_op jit(solution)/shard_map/ppermute | solution.py:75
  70.7 0.0 collective-permute-start.8
  70.7 0.0 collective-permute-done.6
  70.7 3.2 %collective-permute-done.7 = bf16[256,128]{0,1:T(8,128)(2,1)S(1)} collective-permute-done((bf16[256,128]{0,1:T(8,128)(2,1)S(1)}, bf16[256,128]{0,1:T(8,128)(2,1)S(1)}, u32[]{:S(2)}, u32[]{:S(2)}) %collective-permute-start.7) | collective-permute-done | bytes 65568 | tf_op jit(solution)/shard_map/ppermute | solution.py:75
  73.9 1.8 %collective-permute-done.8 = bf16[256,128]{0,1:T(8,128)(2,1)S(1)} collective-permute-done((bf16[256,128]{0,1:T(8,128)(2,1)S(1)}, bf16[256,128]{0,1:T(8,128)(2,1)S(1)}, u32[]{:S(2)}, u32[]{:S(2)}) %collective-permute-start.8) | collective-permute-done | bytes 65568 | tf_op jit(solution)/shard_map/ppermute | solution.py:75
  75.9 2.5 %collective-permute-start.9 = (bf16[256,256]{0,1:T(8,128)(2,1)S(1)}, bf16[256,256]{0,1:T(8,128)(2,1)S(1)}, u32[]{:S(2)}, u32[]{:S(2)}) collective-permute-start(bf16[256,256]{0,1:T(8,128)(2,1)S(1)} %pad_maximum_fusion.1), channel_id=1, source_target_pairs={{0,48},{16,0},{32,16},{48,32},{1,49},{17,1},{33,17},{49,33},{2,50}... | collective-permute-start | bytes 393224 | tf_op jit(solution)/shard_map/ppermute | solution.py:75
  78.4 0.8 fusion.9
  79.2 0.5 collective-permute-start.10
  79.7 0.8 collective-permute-start.11
  80.5 0.8 copy.20
  81.4 3.3 %collective-permute-done.10 = bf16[256,256]{0,1:T(8,128)(2,1)S(1)} collective-permute-done((bf16[256,256]{0,1:T(8,128)(2,1)S(1)}, bf16[256,256]{0,1:T(8,128)(2,1)S(1)}, u32[]{:S(2)}, u32[]{:S(2)}) %collective-permute-start.10) | collective-permute-done | bytes 131104 | tf_op jit(solution)/shard_map/ppermute | solution.py:75
  84.7 3.3 %collective-permute-done.11 = bf16[256,256]{0,1:T(8,128)(2,1)S(1)} collective-permute-done((bf16[256,256]{0,1:T(8,128)(2,1)S(1)}, bf16[256,256]{0,1:T(8,128)(2,1)S(1)}, u32[]{:S(2)}, u32[]{:S(2)}) %collective-permute-start.11) | collective-permute-done | bytes 131104 | tf_op jit(solution)/shard_map/ppermute | solution.py:75
  88.1 0.2 copy.15
  88.3 0.6 slice-done
  88.9 0.7 fusion
  89.6 0.8 fusion.1
  90.5 1.0 %fusion.13 = bf16[256,3,128]{0,2,1:T(8,128)(2,1)S(1)} fusion(f32[1024,256,3]{1,0,2:T(8,128)S(1)} %get-tuple-element.16, f32[3,256]{1,0:T(4,128)S(1)} %broadcast_maximum_fusion, pred[256,1024]{0,1:T(8,128)(4,1)S(1)} %fusion.9, bf16[1024,256]{1,0:T(8,128)(2,1)S(1)} %bitcast.97, f32[256,3]{0,1:T(4,128)S(1)} %bitcast.99), kind=kOutput, calls=%fused_computation.15 | convolution fusion | flops 205455360 | bytes 3874816 | tf_op jit(solution)/shard_map/hqk,kd->hqd/dot_general | solution.py:57
  91.4 0.8 copy.19
  (43 shorter events, 0.4 us)
Async XLA Ops:
  0.6 5.4 %copy-start = (bf16[64,16,384]{2,1,0:T(8,128)(2,1)S(1)}, bf16[64,16,384]{2,1,0:T(8,128)(2,1)}, u32[]{:S(2)}) copy-start(bf16[64,16,384]{2,1,0:T(8,128)(2,1)} %param.11) | copy-start | bytes 2359300
  0.6 22.2 %collective-permute-start = (bf16[256,384]{1,0:T(8,128)(2,1)}, bf16[256,384]{1,0:T(8,128)(2,1)S(1)}, u32[]{:S(2)}, u32[]{:S(2)}) collective-permute-start(bf16[256,384]{1,0:T(8,128)(2,1)} %param.7), channel_id=1, source_target_pairs={{0,192},{64,0},{128,64},{192,128},{1,193},{65,1},{129,65},{193,129... | collective-permute-start | bytes 589832 | tf_op jit(solution)/shard_map/ppermute | solution.py:75
  4.3 19.3 %collective-permute-start.1 = (bf16[256,384]{1,0:T(8,128)(2,1)}, bf16[256,384]{1,0:T(8,128)(2,1)S(1)}, u32[]{:S(2)}, u32[]{:S(2)}) collective-permute-start(bf16[256,384]{1,0:T(8,128)(2,1)} %param.7), channel_id=1, source_target_pairs={{0,128},{64,192},{128,0},{192,64},{1,129},{65,193},{129,1},{193,65... | collective-permute-start | bytes 589832 | tf_op jit(solution)/shard_map/ppermute | solution.py:75
  4.6 19.6 %collective-permute-start.2 = (bf16[256,384]{1,0:T(8,128)(2,1)}, bf16[256,384]{1,0:T(8,128)(2,1)S(1)}, u32[]{:S(2)}, u32[]{:S(2)}) collective-permute-start(bf16[256,384]{1,0:T(8,128)(2,1)} %param.7), channel_id=1, source_target_pairs={{0,64},{64,128},{128,192},{192,0},{1,65},{65,129},{129,193},{193,1... | collective-permute-start | bytes 589832 | tf_op jit(solution)/shard_map/ppermute | solution.py:75
  6.7 12.8 %copy-start.3 = (bf16[256,384]{1,0:T(8,128)(2,1)S(1)}, bf16[256,384]{1,0:T(8,128)(2,1)}, u32[]{:S(2)}) copy-start(bf16[256,384]{1,0:T(8,128)(2,1)} %param.7) | copy-start | bytes 589828
  8.4 11.7 %copy-start.5 = (s32[16,8]{0,1:T(8,128)S(1)}, s32[16,8]{0,1:T(8,128)}, u32[]{:S(2)}) copy-start(s32[16,8]{0,1:T(8,128)} %param.13) | copy-start | bytes 1540
  8.5 11.7 %copy-start.6 = (s32[16,8]{0,1:T(8,128)S(1)}, s32[16,8]{0,1:T(8,128)}, u32[]{:S(2)}) copy-start(s32[16,8]{0,1:T(8,128)} %param.12) | copy-start | bytes 1540
  9.5 24.5 %all-to-all-start = ((bf16[16,32,384]{2,1,0:T(8,128)(2,1)}), bf16[16,32,384]{2,1,0:T(8,128)(2,1)S(1)}, u32[]{:S(2)}, u32[]{:S(2)}) async-start(bf16[16,32,384]{2,1,0:T(8,128)(2,1)} %pad_maximum_fusion), calls=%async_computation | async-start | bytes 786432 | tf_op jit(solution)/shard_map/all_to_all | solution.py:135
  28.9 5.6 %copy-start.1 = (bf16[4,256,384]{2,1,0:T(8,128)(2,1)}, bf16[4,256,384]{2,1,0:T(8,128)(2,1)S(1)}, u32[]{:S(2)}) copy-start(bf16[4,256,384]{2,1,0:T(8,128)(2,1)S(1)} %constant_dynamic-slice_fusion.8) | copy-start | bytes 2359300
  34.0 1.4 %copy-start.4 = (bf16[384,384]{1,0:T(8,128)(2,1)S(1)}, bf16[384,384]{1,0:T(8,128)(2,1)}, u32[]{:S(2)}) copy-start(bf16[384,384]{1,0:T(8,128)(2,1)} %param.8) | copy-start | bytes 884740
  38.4 14.9 %collective-permute-start.3 = (f32[256,512]{0,1:T(8,128)}, f32[256,512]{0,1:T(8,128)}, u32[]{:S(2)}, u32[]{:S(2)}) collective-permute-start(f32[256,512]{0,1:T(8,128)} %get-tuple-element.8), channel_id=1, source_target_pairs={{0,16},{16,32},{32,48},{48,0},{1,17},{17,33},{33,49},{49,1},{2,18}... | collective-permute-start | bytes 1572872 | tf_op jit(solution)/shard_map/ppermute | solution.py:99
  39.7 25.9 %collective-permute-start.4 = (f32[256,512]{0,1:T(8,128)}, f32[256,512]{0,1:T(8,128)}, u32[]{:S(2)}, u32[]{:S(2)}) collective-permute-start(f32[256,512]{0,1:T(8,128)} %get-tuple-element.10), channel_id=1, source_target_pairs={{0,32},{16,48},{32,0},{48,16},{1,33},{17,49},{33,1},{49,17},{2,34}... | collective-permute-start | bytes 1572872 | tf_op jit(solution)/shard_map/ppermute | solution.py:99
  42.1 23.6 %collective-permute-start.5 = (f32[256,512]{0,1:T(8,128)S(1)}, f32[256,512]{0,1:T(8,128)}, u32[]{:S(2)}, u32[]{:S(2)}) collective-permute-start(f32[256,512]{0,1:T(8,128)S(1)} %get-tuple-element.9), channel_id=1, source_target_pairs={{0,48},{16,0},{32,16},{48,32},{1,49},{17,1},{33,17},{49,33},{2,50}... | collective-permute-start | bytes 1572872 | tf_op jit(solution)/shard_map/ppermute | solution.py:99
  67.2 17.5 %copy-start.2 = (bf16[256,512]{0,1:T(8,128)(2,1)}, bf16[256,512]{0,1:T(8,128)(2,1)S(1)}, u32[]{:S(2)}) copy-start(bf16[256,512]{0,1:T(8,128)(2,1)S(1)} %add_convert_fusion) | copy-start | bytes 786436
  67.2 3.5 %collective-permute-start.6 = (bf16[256,128]{0,1:T(8,128)(2,1)S(1)}, bf16[256,128]{0,1:T(8,128)(2,1)S(1)}, u32[]{:S(2)}, u32[]{:S(2)}) collective-permute-start(bf16[256,128]{0,1:T(8,128)(2,1)S(1)} %slice.24), channel_id=1, source_target_pairs={{0,192},{64,0},{128,64},{192,128},{1,193},{65,1},{129,65},{193,129... | collective-permute-start | bytes 196616 | tf_op jit(solution)/shard_map/ppermute | solution.py:75
  69.3 4.6 %collective-permute-start.7 = (bf16[256,128]{0,1:T(8,128)(2,1)S(1)}, bf16[256,128]{0,1:T(8,128)(2,1)S(1)}, u32[]{:S(2)}, u32[]{:S(2)}) collective-permute-start(bf16[256,128]{0,1:T(8,128)(2,1)S(1)} %slice.24), channel_id=1, source_target_pairs={{0,128},{64,192},{128,0},{192,64},{1,129},{65,193},{129,1},{193,65... | collective-permute-start | bytes 196616 | tf_op jit(solution)/shard_map/ppermute | solution.py:75
  70.7 5.0 %collective-permute-start.8 = (bf16[256,128]{0,1:T(8,128)(2,1)S(1)}, bf16[256,128]{0,1:T(8,128)(2,1)S(1)}, u32[]{:S(2)}, u32[]{:S(2)}) collective-permute-start(bf16[256,128]{0,1:T(8,128)(2,1)S(1)} %slice.24), channel_id=1, source_target_pairs={{0,64},{64,128},{128,192},{192,0},{1,65},{65,129},{129,193},{193,1... | collective-permute-start | bytes 196616 | tf_op jit(solution)/shard_map/ppermute | solution.py:75
  75.9 5.4 %collective-permute-start.9 = (bf16[256,256]{0,1:T(8,128)(2,1)S(1)}, bf16[256,256]{0,1:T(8,128)(2,1)S(1)}, u32[]{:S(2)}, u32[]{:S(2)}) collective-permute-start(bf16[256,256]{0,1:T(8,128)(2,1)S(1)} %pad_maximum_fusion.1), channel_id=1, source_target_pairs={{0,48},{16,0},{32,16},{48,32},{1,49},{17,1},{33,17},{49,33},{2,50}... | collective-permute-start | bytes 393224 | tf_op jit(solution)/shard_map/ppermute | solution.py:75
  79.2 5.5 %collective-permute-start.10 = (bf16[256,256]{0,1:T(8,128)(2,1)S(1)}, bf16[256,256]{0,1:T(8,128)(2,1)S(1)}, u32[]{:S(2)}, u32[]{:S(2)}) collective-permute-start(bf16[256,256]{0,1:T(8,128)(2,1)S(1)} %pad_maximum_fusion.1), channel_id=1, source_target_pairs={{0,32},{16,48},{32,0},{48,16},{1,33},{17,49},{33,1},{49,17},{2,34}... | collective-permute-start | bytes 393224 | tf_op jit(solution)/shard_map/ppermute | solution.py:75
  79.7 8.3 %collective-permute-start.11 = (bf16[256,256]{0,1:T(8,128)(2,1)S(1)}, bf16[256,256]{0,1:T(8,128)(2,1)S(1)}, u32[]{:S(2)}, u32[]{:S(2)}) collective-permute-start(bf16[256,256]{0,1:T(8,128)(2,1)S(1)} %pad_maximum_fusion.1), channel_id=1, source_target_pairs={{0,16},{16,32},{32,48},{48,0},{1,17},{17,33},{33,49},{49,1},{2,18}... | collective-permute-start | bytes 393224 | tf_op jit(solution)/shard_map/ppermute | solution.py:75
  88.0 0.9 %slice-start = ((bf16[256,512]{0,1:T(8,128)(2,1)}), bf16[256,384]{0,1:T(8,128)(2,1)S(1)}, s32[]{:S(2)}) async-start(bf16[256,512]{0,1:T(8,128)(2,1)} %copy-done.2), calls=%async_computation.1 | async-start | bytes 393216 | tf_op jit(solution)/shard_map/slice | solution.py:159

commit v5 on v4

--- a/solution.py
+++ b/solution.py
@@ -102,21 +102,32 @@
 
 def body(hidden_states, w_query, w_key_value, adapter_down, adapter_up, req_lengths, req_adapter):
     dp_size = lax.axis_size("dp")
+    row_size = lax.axis_size("row")
+    col_size = lax.axis_size("col")
     block_index = lax.axis_index("dp")
     col_index = lax.axis_index("col")
     row_index = lax.axis_index("row")
-    gathered = ring_gather(hidden_states, "row", 0)
-    block_len = gathered.shape[0]
+    own_rows = hidden_states.shape[0]
+    block_len = own_rows * row_size
     query_cols = w_query.shape[1]
     kv_cols = w_key_value.shape[1]
     kv_half = kv_cols // 2
     head_size = HEAD_DIM
     heads_here = query_cols // head_size
-    heads_total = heads_here * lax.axis_size("row")
+    heads_total = heads_here * row_size
     kv_heads = kv_half // head_size
     kv_group = row_index * heads_here // (heads_total // kv_heads)
-    own_rows = block_len // lax.axis_size("col")
     first_row = col_index * own_rows
+
+    key_cols = lax.dynamic_slice_in_dim(w_key_value, kv_group * head_size, head_size, 1)
+    value_cols = lax.dynamic_slice_in_dim(w_key_value, kv_half + kv_group * head_size, head_size, 1)
+    weight_piece = jnp.concatenate([w_query, key_cols, value_cols], axis=1)
+    weights_full = ring_gather(weight_piece, "col", 0)
+
+    grid = [(a * col_size + b, b * col_size + a) for a in range(row_size) for b in range(col_size)]
+    swapped = lax.ppermute(hidden_states, ("row", "col"), grid)
+    own_inputs = ring_gather(swapped, "row", 1)
+
     held_sets = adapter_down.shape[0]
     width_here = adapter_down.shape[1]
     rank_size = adapter_down.shape[2]
@@ -124,9 +135,11 @@
     adapters_row = req_adapter[block_index]
     requests = lengths_row.shape[0]
     starts, segment, positions = block_layout(lengths_row, block_len)
-    request_of = jnp.clip(segment - 1, 0, requests - 1)
-    in_request = segment > 0
     holders = adapters_row // held_sets
+    request_ids = jnp.arange(requests, dtype=jnp.int32)
+    token_holder = jnp.sum(
+        jnp.where(segment[:, None] == request_ids[None, :] + 1, holders[None, :] + 1, 0), axis=1
+    ) - 1
     wanted_from_me = (req_adapter // held_sets) == block_index
     local_pick = jnp.sum(jnp.where(wanted_from_me, req_adapter % held_sets, 0), axis=1)
     down_pick = jnp.transpose(jnp.take(adapter_down, local_pick, axis=0), (0, 2, 1))
@@ -135,36 +148,40 @@
     incoming = lax.all_to_all(outgoing, "dp", split_axis=0, concat_axis=0, tiled=True)
     flat_down = incoming[:, :rank_size, :].reshape(dp_size * rank_size, width_here).T
     flat_up = incoming[:, rank_size:, :].reshape(dp_size * rank_size, query_cols).astype(jnp.float32)
-    rank_owner = jnp.arange(dp_size * rank_size, dtype=jnp.int32) // rank_size
-    reduced = jnp.dot(gathered, flat_down, preferred_element_type=jnp.float32)
-    request_ids = jnp.arange(requests, dtype=jnp.int32)
-    token_holder = jnp.sum(
-        jnp.where(segment[:, None] == request_ids[None, :] + 1, holders[None, :] + 1, 0), axis=1
-    ) - 1
-    kept_cols = rank_owner[None, :] == token_holder[:, None]
-    reduced = jnp.where(kept_cols, reduced, 0.0)
-    adapter_term = jnp.dot(reduced, flat_up, precision=lax.Precision.HIGHEST)
-    kv_share = kv_cols // lax.axis_size("row")
-    kv_slice = lax.dynamic_slice_in_dim(w_key_value, row_index * kv_share, kv_share, 1)
-    both_weights = jnp.concatenate([w_query, kv_slice], axis=1)
-    partial_value = jnp.dot(gathered, both_weights, preferred_element_type=jnp.float32)
-    summed = ring_reduce_scatter(
-        partial_value
-        + jnp.concatenate(
-            [adapter_term, jnp.zeros((own_rows * lax.axis_size("col"), kv_share), jnp.float32)],
-            axis=1,
-        ),
-        "col",
-    )
-    query_rows = summed[:, :query_cols].astype(jnp.bfloat16)
-    kv_cache = ring_gather(summed[:, query_cols:].astype(jnp.bfloat16), "row", 1)
-    head_kv = jnp.concatenate(
-        [
-            lax.dynamic_slice_in_dim(kv_cache, kv_group * head_size, head_size, 1),
-            lax.dynamic_slice_in_dim(kv_cache, kv_half + kv_group * head_size, head_size, 1),
-        ],
+    slot_ids = jnp.arange(dp_size, dtype=jnp.int32)
+
+    local_holder = lax.dynamic_slice_in_dim(token_holder, row_index * own_rows, own_rows, 0)
+    reduced = jnp.dot(hidden_states, flat_down, preferred_element_type=jnp.float32)
+    reduced = reduced.reshape(own_rows, dp_size, rank_size)
+    local_mask = slot_ids[None, :] == local_holder[:, None]
+    low_partial = jnp.sum(jnp.where(local_mask[:, :, None], reduced, 0.0), axis=1)
+    low_swapped = lax.ppermute(low_partial, ("row", "col"), grid)
+    low_rank = sum(shifted_copies(low_swapped, "row"))
+
+    own_holder = lax.dynamic_slice_in_dim(token_holder, first_row, own_rows, 0)
+    own_mask = slot_ids[None, :] == own_holder[:, None]
+    spread = jnp.where(own_mask[:, :, None], low_rank[:, None, :], 0.0)
+    spread = spread.reshape(own_rows, dp_size * rank_size)
+    adapter_term = jnp.dot(spread, flat_up, precision=lax.Precision.HIGHEST)
+
+    query_rows = (
+        jnp.dot(own_inputs, weights_full[:, :query_cols], preferred_element_type=jnp.float32)
+        + adapter_term
+    ).astype(jnp.bfloat16)
+    head_kv = jnp.dot(
+        own_inputs, weights_full[:, query_cols:], preferred_element_type=jnp.float32
+    ).astype(jnp.bfloat16)
+
+    partner = [(i, (i + row_size // kv_heads) % row_size) for i in range(row_size)]
+    other_kv = lax.ppermute(head_kv, "row", partner)
+    first_is_own = kv_group == 0
+    low_head = jnp.where(first_is_own, head_kv, other_kv)
+    high_head = jnp.where(first_is_own, other_kv, head_kv)
+    kv_cache = jnp.concatenate(
+        [low_head[:, :head_size], high_head[:, :head_size], low_head[:, head_size:], high_head[:, head_size:]],
         axis=1,
     )
+
     attend, initial = make_attend(query_rows, segment, first_row, 0, head_size, head_size)
     running_max, running_sum, running_out = attend(
         initial, ring_gather(head_kv, "col", 0), jnp.int32(0)

time: 92.6 us -> 99.2 us (1.071)
  the two profiles are of different devices: /device:TPU:1 before, /device:TPU:160 now
where the time goes in v5:
time: 99.2 us; the launch traced here: 98.5 us
  starting transfers between devices  42.9 us (43%)
  waiting for transfers between devices  24.8 us (25%)
  local copies, waits for them, and re-layouts  13.2 us (13%)
  other arithmetic  10.8 us (11%)
  matrix products  5.03 us (5%)
  between operations  1.84 us (2%)
    ppermute x12, starting transfers between devices, shifted_copies(): copies.append(lax.ppermute(x, axis_name, perm))  31.6 us
    ppermute x12, waiting for transfers between devices, shifted_copies(): copies.append(lax.ppermute(x, axis_name, perm))  24.8 us
    all_to_all x1, starting transfers between devices, body(): lax.all_to_all(outgoing, 'dp', split_axis=0, concat_axis=0, tiled=True)  6.77 us
    unnamed x48, local copies, waits for them, and re-layouts  6.11 us
    ppermute x1, starting transfers between devices, body(): swapped = lax.ppermute(hidden_states, ('row', 'col'), grid)  3 us
    dynamic_slice x3, local copies, waits for them, and re-layouts, ring_gather(): ordered = lax.dynamic_slice_in_dim(doubled, size - me, size, 0)  2.14 us
  transfers between devices with their start and end apart: 16, of which 6 were waited for; matrix products, arithmetic and copies ran while one was open for 18% of the time, Pallas kernels for 0%

profile of v5, /device:TPU:160, one launch (start us, length us, event | category | flops | bytes accessed | tf_op | source)
XLA Modules:
  0.0 98.5 jit_solution(13686182857666685846)
XLA Ops:
  0.6 0.0 copy-start
  0.7 1.1 %constant_dynamic-slice_fusion.3 = (bf16[384,128]{1,0:T(8,128)(2,1)S(1)}, bf16[384,128]{1,0:T(8,128)(2,1)S(1)}) fusion(bf16[384,512]{1,0:T(8,128)(2,1)} %param.9, s32[]{:T(128)S(6)} %select_n.115, s32[]{:T(128)S(6)} %select_n.116), kind=kLoop, calls=%fused_computation.97 | loop fusion | bytes 393224 | tf_op jit(solution)/shard_map/dynamic_slice | solution.py:122
  1.8 1.9 %pad_maximum_fusion = bf16[384,640]{1,0:T(8,128)(2,1)} fusion(bf16[384,128]{1,0:T(8,128)(2,1)S(1)} %get-tuple-element.11, bf16[384,128]{1,0:T(8,128)(2,1)S(1)} %get-tuple-element.10, bf16[384,384]{1,0:T(8,128)(2,1)} %param.8), kind=kLoop, calls=%fused_computation.20 | loop fusion | flops 1474560 | bytes 983040 | tf_op jit(solution)/shard_map/concatenate | solution.py:124
  3.7 2.8 %collective-permute-start.4 = (bf16[384,640]{1,0:T(8,128)(2,1)}, bf16[384,640]{1,0:T(8,128)(2,1)S(1)}, u32[]{:S(2)}, u32[]{:S(2)}) collective-permute-start(bf16[384,640]{1,0:T(8,128)(2,1)} %pad_maximum_fusion), channel_id=1, source_target_pairs={{0,48},{16,0},{32,16},{48,32},{1,49},{17,1},{33,17},{49,33},{2,50}... | collective-permute-start | bytes 1474568 | tf_op jit(solution)/shard_map/ppermute | solution.py:75
  6.4 0.8 collective-permute-start.5
  7.2 0.9 collective-permute-start.6
  8.1 1.7 %copy.19 = bf16[256,384]{0,1:T(8,128)(2,1)} copy(bf16[256,384]{1,0:T(8,128)(2,1)} %param.7) | data formatting | bytes 393216 | tf_op args[0]
  9.9 3.0 %collective-permute-start = (bf16[256,384]{0,1:T(8,128)(2,1)}, bf16[256,384]{0,1:T(8,128)(2,1)}, u32[]{:S(2)}, u32[]{:S(2)}) collective-permute-start(bf16[256,384]{0,1:T(8,128)(2,1)} %copy.19), channel_id=1, source_target_pairs={{0,0},{16,64},{32,128},{48,192},{64,16},{80,80},{96,144},{112,208}... | collective-permute-start | bytes 589832 | tf_op jit(solution)/shard_map/ppermute | solution.py:128
  12.9 0.7 fusion.32
  13.6 1.3 %gather_fusion.1 = bf16[16,16,384]{2,1,0:T(8,128)(2,1)} fusion(bf16[64,16,384]{2,1,0:T(8,128)(2,1)S(1)} %copy-done, s32[1024]{0:T(1024)S(1)} %pad_clamp_fusion), kind=kCustom, calls=%fused_computation.1 | custom fusion | bytes 393280 | tf_op jit(solution)/shard_map/jit(_take)/gather | solution.py:146
  14.9 0.6 gather_fusion
  15.5 1.0 %broadcast_select_fusion = bf16[16,16,384]{2,1,0:T(8,128)(2,1)S(1)} fusion(bf16[16,16,384]{2,1,0:T(8,128)(2,1)} %gather_fusion.1, pred[16]{0:T(512)(128)(4,1)S(1)} %compare_and_fusion), kind=kLoop, calls=%fused_computation.46 | loop fusion | flops 98304 | bytes 393232 | tf_op jit(solution)/shard_map/jit(_take)/select_n | solution.py:146
  16.5 0.1 select_bitcast_fusion
  16.6 0.8 pad_maximum_fusion.1
  17.4 6.8 %all-to-all-start = ((bf16[16,32,384]{2,1,0:T(8,128)(2,1)}), bf16[16,32,384]{2,1,0:T(8,128)(2,1)S(1)}, u32[]{:S(2)}, u32[]{:S(2)}) async-start(bf16[16,32,384]{2,1,0:T(8,128)(2,1)} %pad_maximum_fusion.1), calls=%async_computation | async-start | bytes 786432 | tf_op jit(solution)/shard_map/all_to_all | solution.py:148
  24.2 1.8 %bitcast_dynamic-update-slice_fusion.6 = bf16[8,384,640]{2,1,0:T(8,128)(2,1)} fusion(bf16[384,128]{1,0:T(8,128)(2,1)} %copy-done.5, bf16[384,128]{1,0:T(8,128)(2,1)} %copy-done.3, bf16[384,384]{1,0:T(8,128)(2,1)S(1)} %copy-done.2), kind=kLoop, calls=%fused_computation.27 | loop fusion | flops 1474559 | bytes 983040
  26.0 0.7 fusion.41
  27.4 0.1 subtract_reduce_fusion
  27.5 0.1 convert_reduce_fusion
  27.6 0.1 select_reduce_fusion.1
  27.7 0.1 dynamic_slice.37
  27.8 0.1 fusion.44
  27.9 0.8 fusion.13
  28.7 13.9 %collective-permute-start.1 = (bf16[256,384]{0,1:T(8,128)(2,1)}, bf16[256,384]{0,1:T(8,128)(2,1)S(1)}, u32[]{:S(2)}, u32[]{:S(2)}) collective-permute-start(bf16[256,384]{0,1:T(8,128)(2,1)} %collective-permute-done), channel_id=1, source_target_pairs={{0,192},{64,0},{128,64},{192,128},{1,193},{65,1},{129,65},{193,129... | collective-permute-start | bytes 589832 | tf_op jit(solution)/shard_map/ppermute | solution.py:75
  42.6 0.0 collective-permute-start.2
  42.6 1.0 %bitcast_dynamic-update-slice_fusion.14 = bf16[8,256,384]{1,2,0:T(8,128)(2,1)S(1)} fusion(bf16[256,384]{0,1:T(8,128)(2,1)} %collective-permute-done), kind=kLoop, calls=%fused_computation.43 | loop fusion | bytes 393216
  43.6 7.9 %collective-permute-done.1 = bf16[256,384]{0,1:T(8,128)(2,1)S(1)} collective-permute-done((bf16[256,384]{0,1:T(8,128)(2,1)}, bf16[256,384]{0,1:T(8,128)(2,1)S(1)}, u32[]{:S(2)}, u32[]{:S(2)}) %collective-permute-start.1) | collective-permute-done | bytes 196640 | tf_op jit(solution)/shard_map/ppermute | solution.py:75
  51.5 8.5 %collective-permute-done.3 = bf16[256,384]{0,1:T(8,128)(2,1)S(1)} collective-permute-done((bf16[256,384]{0,1:T(8,128)(2,1)}, bf16[256,384]{0,1:T(8,128)(2,1)S(1)}, u32[]{:S(2)}, u32[]{:S(2)}) %collective-permute-start.3) | collective-permute-done | bytes 196640 | tf_op jit(solution)/shard_map/ppermute | solution.py:75
  60.1 1.0 bitcast_dynamic-update-slice_fusion.15
  61.1 0.1 constant_dynamic-slice_fusion.4
  61.2 0.1 bitcast_dynamic-update-slice_fusion.4
  61.3 0.1 bitcast_dynamic-update-slice_fusion.2
  61.4 0.1 bitcast_dynamic-update-slice_fusion
  61.5 0.1 bitcast_dynamic-update-slice_fusion.7
  61.5 0.1 bitcast_dynamic-update-slice_fusion.5
  61.6 0.1 bitcast_dynamic-update-slice_fusion.3
  61.7 0.1 bitcast_dynamic-update-slice_fusion.1
  61.7 0.2 constant_dynamic-slice_fusion.1
  61.9 0.2 copy-done.8
  62.1 0.4 bitcast_dynamic-update-slice_fusion.22
  62.5 0.1 collective-permute-start.7
  62.6 0.9 collective-permute-start.14
  63.5 0.2 collective-permute-start.8
  63.7 1.7 %collective-permute-start.9 = (bf16[256,256]{1,0:T(8,128)(2,1)S(1)}, bf16[256,256]{1,0:T(8,128)(2,1)S(1)}, u32[]{:S(2)}, u32[]{:S(2)}) collective-permute-start(bf16[256,256]{1,0:T(8,128)(2,1)S(1)} %get-tuple-element.21), channel_id=1, source_target_pairs={{0,16},{16,32},{32,48},{48,0},{1,17},{17,33},{33,49},{49,1},{2,18}... | collective-permute-start | bytes 393224 | tf_op jit(solution)/shard_map/ppermute | solution.py:75
  65.5 3.1 %collective-permute-done.7 = bf16[256,256]{1,0:T(8,128)(2,1)S(1)} collective-permute-done((bf16[256,256]{1,0:T(8,128)(2,1)S(1)}, bf16[256,256]{1,0:T(8,128)(2,1)S(1)}, u32[]{:S(2)}, u32[]{:S(2)}) %collective-permute-start.7) | collective-permute-done | bytes 131104 | tf_op jit(solution)/shard_map/ppermute | solution.py:75
  68.5 2.4 %collective-permute-done.8 = bf16[256,256]{1,0:T(8,128)(2,1)S(1)} collective-permute-done((bf16[256,256]{1,0:T(8,128)(2,1)S(1)}, bf16[256,256]{1,0:T(8,128)(2,1)S(1)}, u32[]{:S(2)}, u32[]{:S(2)}) %collective-permute-start.8) | collective-permute-done | bytes 131104 | tf_op jit(solution)/shard_map/ppermute | solution.py:75
  71.0 0.9 collective-permute-done.9
  72.1 0.9 copy-done.11
  73.0 0.7 fusion.42
  73.7 1.2 %fusion.45 = f32[256,256]{1,0:T(8,128)S(1)} fusion(bf16[256,384]{1,0:T(8,128)(2,1)S(1)} %bitcast.97, bf16[256,384]{1,0:T(8,128)(2,1)} %param.7), kind=kOutput, calls=%fused_computation.111 | convolution fusion | flops 50331648 | bytes 655360 | tf_op jit(solution)/shard_map/dot_general | solution.py:154
  75.0 0.7 collective-permute-start.10
  75.7 1.9 %constant_dynamic-slice_fusion = bf16[4,256,256]{2,1,0:T(8,128)(2,1)} fusion(bf16[8,256,256]{2,1,0:T(8,128)(2,1)} %copy-done.11, s32[]{:T(128)S(6)} %select_n.117), kind=kLoop, calls=%fused_computation.94 | loop fusion | bytes 1048580 | tf_op jit(solution)/shard_map/dynamic_slice | solution.py:84
  77.6 7.6 %collective-permute-start.11 = (f32[256,16]{0,1:T(8,128)S(1)}, f32[256,16]{0,1:T(8,128)S(1)}, u32[]{:S(2)}, u32[]{:S(2)}) collective-permute-start(f32[256,16]{0,1:T(8,128)S(1)} %collective-permute-done.10), channel_id=1, source_target_pairs={{0,192},{64,0},{128,64},{192,128},{1,193},{65,1},{129,65},{193,129... | collective-permute-start | bytes 49160 | tf_op jit(solution)/shard_map/ppermute | solution.py:75
  85.1 2.3 %collective-permute-start.12 = (f32[256,16]{0,1:T(8,128)S(1)}, f32[256,16]{0,1:T(8,128)S(1)}, u32[]{:S(2)}, u32[]{:S(2)}) collective-permute-start(f32[256,16]{0,1:T(8,128)S(1)} %collective-permute-done.10), channel_id=1, source_target_pairs={{0,128},{64,192},{128,0},{192,64},{1,129},{65,193},{129,1},{193,65... | collective-permute-start | bytes 49160 | tf_op jit(solution)/shard_map/ppermute | solution.py:75
  87.4 1.4 %collective-permute-start.13 = (f32[256,16]{0,1:T(8,128)S(1)}, f32[256,16]{0,1:T(8,128)S(1)}, u32[]{:S(2)}, u32[]{:S(2)}) collective-permute-start(f32[256,16]{0,1:T(8,128)S(1)} %collective-permute-done.10), channel_id=1, source_target_pairs={{0,64},{64,128},{128,192},{192,0},{1,65},{65,129},{129,193},{193,1... | collective-permute-start | bytes 49160 | tf_op jit(solution)/shard_map/ppermute | solution.py:75
  88.8 1.6 %pad_maximum_fusion.2 = bf16[256,512]{1,0:T(8,128)(2,1)} fusion(bf16[256,128]{1,0:T(8,128)(2,1)} %get-tuple-element.25, bf16[256,128]{1,0:T(8,128)(2,1)S(1)} %get-tuple-element.15, bf16[256,128]{1,0:T(8,128)(2,1)} %get-tuple-element.26, bf16[256,128]{1,0:T(8,128)(2,1)S(1)} %get-tuple-element.14), kind=kLoop, calls=%fused_computation.33 | loop fusion | flops 1048576 | bytes 524288 | tf_op jit(solution)/shard_map/concatenate | solution.py:180
  90.5 1.9 %collective-permute-done.13 = f32[256,16]{0,1:T(8,128)S(1)} collective-permute-done((f32[256,16]{0,1:T(8,128)S(1)}, f32[256,16]{0,1:T(8,128)S(1)}, u32[]{:S(2)}, u32[]{:S(2)}) %collective-permute-start.13) | collective-permute-done | bytes 16416 | tf_op jit(solution)/shard_map/ppermute | solution.py:75
  92.4 0.4 convolution_bitcast_fusion
  92.8 1.3 %fusion.10 = bf16[256,384]{1,0:T(8,128)(2,1)} fusion(f32[256,384]{1,0:T(8,128)S(1)} %convolution_bitcast_fusion, bf16[256,1536]{0,1:T(8,128)(2,1)S(1)} %bitcast.96, bf16[1536,640]{1,0:T(8,128)(2,1)S(1)} %bitcast.93), kind=kOutput, calls=%fused_computation.13 | convolution fusion | flops 302186496 | bytes 2555904 | tf_op jit(solution)/shard_map/dot_general | solution.py:168
  94.1 1.1 %copy.20 = bf16[256,384]{0,1:T(8,128)(2,1)S(1)} copy(bf16[256,384]{1,0:T(8,128)(2,1)} %fusion.10) | data formatting | bytes 393216 | tf_op jit(solution)/shard_map/convert_element_type | solution.py:170
  95.2 0.7 fusion
  95.9 0.8 fusion.1
  96.7 1.0 fusion.17
  97.7 0.8 copy.24
  (64 shorter events, 0.4 us)
Async XLA Ops:
  0.6 13.0 %copy-start = (bf16[64,16,384]{2,1,0:T(8,128)(2,1)S(1)}, bf16[64,16,384]{2,1,0:T(8,128)(2,1)}, u32[]{:S(2)}) copy-start(bf16[64,16,384]{2,1,0:T(8,128)(2,1)} %param.11) | copy-start | bytes 2359300
  0.6 14.2 %copy-start.1 = (bf16[64,384,16]{1,2,0:T(8,128)(2,1)S(1)}, bf16[64,384,16]{1,2,0:T(8,128)(2,1)}, u32[]{:S(2)}) copy-start(bf16[64,384,16]{1,2,0:T(8,128)(2,1)} %param.10) | copy-start | bytes 2359300
  1.8 4.7 %copy-start.3 = (bf16[384,128]{1,0:T(8,128)(2,1)}, bf16[384,128]{1,0:T(8,128)(2,1)S(1)}, u32[]{:S(2)}) copy-start(bf16[384,128]{1,0:T(8,128)(2,1)S(1)} %get-tuple-element.10) | copy-start | bytes 294916
  1.8 4.7 %copy-start.5 = (bf16[384,128]{1,0:T(8,128)(2,1)}, bf16[384,128]{1,0:T(8,128)(2,1)S(1)}, u32[]{:S(2)}) copy-start(bf16[384,128]{1,0:T(8,128)(2,1)S(1)} %get-tuple-element.11) | copy-start | bytes 294916
  3.7 20.5 %copy-start.2 = (bf16[384,384]{1,0:T(8,128)(2,1)S(1)}, bf16[384,384]{1,0:T(8,128)(2,1)}, u32[]{:S(2)}) copy-start(bf16[384,384]{1,0:T(8,128)(2,1)} %param.8) | copy-start | bytes 884740
  3.7 57.5 %collective-permute-start.4 = (bf16[384,640]{1,0:T(8,128)(2,1)}, bf16[384,640]{1,0:T(8,128)(2,1)S(1)}, u32[]{:S(2)}, u32[]{:S(2)}) collective-permute-start(bf16[384,640]{1,0:T(8,128)(2,1)} %pad_maximum_fusion), channel_id=1, source_target_pairs={{0,48},{16,0},{32,16},{48,32},{1,49},{17,1},{33,17},{49,33},{2,50}... | collective-permute-start | bytes 1474568 | tf_op jit(solution)/shard_map/ppermute | solution.py:75
  6.4 54.8 %collective-permute-start.5 = (bf16[384,640]{1,0:T(8,128)(2,1)}, bf16[384,640]{1,0:T(8,128)(2,1)S(1)}, u32[]{:S(2)}, u32[]{:S(2)}) collective-permute-start(bf16[384,640]{1,0:T(8,128)(2,1)} %pad_maximum_fusion), channel_id=1, source_target_pairs={{0,32},{16,48},{32,0},{48,16},{1,33},{17,49},{33,1},{49,17},{2,34}... | collective-permute-start | bytes 1474568 | tf_op jit(solution)/shard_map/ppermute | solution.py:75
  7.2 54.1 %collective-permute-start.6 = (bf16[384,640]{1,0:T(8,128)(2,1)}, bf16[384,640]{1,0:T(8,128)(2,1)S(1)}, u32[]{:S(2)}, u32[]{:S(2)}) collective-permute-start(bf16[384,640]{1,0:T(8,128)(2,1)} %pad_maximum_fusion), channel_id=1, source_target_pairs={{0,16},{16,32},{32,48},{48,0},{1,17},{17,33},{33,49},{49,1},{2,18}... | collective-permute-start | bytes 1474568 | tf_op jit(solution)/shard_map/ppermute | solution.py:75
  9.9 18.8 %collective-permute-start = (bf16[256,384]{0,1:T(8,128)(2,1)}, bf16[256,384]{0,1:T(8,128)(2,1)}, u32[]{:S(2)}, u32[]{:S(2)}) collective-permute-start(bf16[256,384]{0,1:T(8,128)(2,1)} %copy.19), channel_id=1, source_target_pairs={{0,0},{16,64},{32,128},{48,192},{64,16},{80,80},{96,144},{112,208}... | collective-permute-start | bytes 589832 | tf_op jit(solution)/shard_map/ppermute | solution.py:128
  14.9 11.1 %copy-start.12 = (s32[16,8]{0,1:T(8,128)S(1)}, s32[16,8]{0,1:T(8,128)}, u32[]{:S(2)}) copy-start(s32[16,8]{0,1:T(8,128)} %param.13) | copy-start | bytes 1540
  14.9 11.1 %copy-start.13 = (s32[16,8]{0,1:T(8,128)S(1)}, s32[16,8]{0,1:T(8,128)}, u32[]{:S(2)}) copy-start(s32[16,8]{0,1:T(8,128)} %param.12) | copy-start | bytes 1540
  17.4 56.3 %all-to-all-start = ((bf16[16,32,384]{2,1,0:T(8,128)(2,1)}), bf16[16,32,384]{2,1,0:T(8,128)(2,1)S(1)}, u32[]{:S(2)}, u32[]{:S(2)}) async-start(bf16[16,32,384]{2,1,0:T(8,128)(2,1)} %pad_maximum_fusion.1), calls=%async_computation | async-start | bytes 786432 | tf_op jit(solution)/shard_map/all_to_all | solution.py:148
  27.8 33.4 %copy-start.7 = (bf16[8,384,640]{2,1,0:T(8,128)(2,1)S(1)}, bf16[8,384,640]{2,1,0:T(8,128)(2,1)}, u32[]{:S(2)}) copy-start(bf16[8,384,640]{2,1,0:T(8,128)(2,1)} %bitcast_dynamic-update-slice_fusion.6) | copy-start | bytes 11796484
  28.7 22.7 %collective-permute-start.1 = (bf16[256,384]{0,1:T(8,128)(2,1)}, bf16[256,384]{0,1:T(8,128)(2,1)S(1)}, u32[]{:S(2)}, u32[]{:S(2)}) collective-permute-start(bf16[256,384]{0,1:T(8,128)(2,1)} %collective-permute-done), channel_id=1, source_target_pairs={{0,192},{64,0},{128,64},{192,128},{1,193},{65,1},{129,65},{193,129... | collective-permute-start | bytes 589832 | tf_op jit(solution)/shard_map/ppermute | solution.py:75
  42.6 8.9 %collective-permute-start.2 = (bf16[256,384]{0,1:T(8,128)(2,1)}, bf16[256,384]{0,1:T(8,128)(2,1)S(1)}, u32[]{:S(2)}, u32[]{:S(2)}) collective-permute-start(bf16[256,384]{0,1:T(8,128)(2,1)} %collective-permute-done), channel_id=1, source_target_pairs={{0,128},{64,192},{128,0},{192,64},{1,129},{65,193},{129,1},{193,65... | collective-permute-start | bytes 589832 | tf_op jit(solution)/shard_map/ppermute | solution.py:75
  51.4 8.6 %collective-permute-start.3 = (bf16[256,384]{0,1:T(8,128)(2,1)}, bf16[256,384]{0,1:T(8,128)(2,1)S(1)}, u32[]{:S(2)}, u32[]{:S(2)}) collective-permute-start(bf16[256,384]{0,1:T(8,128)(2,1)} %collective-permute-done), channel_id=1, source_target_pairs={{0,64},{64,128},{128,192},{192,0},{1,65},{65,129},{129,193},{193,1... | collective-permute-start | bytes 589832 | tf_op jit(solution)/shard_map/ppermute | solution.py:75
  60.0 1.4 %copy-start.4 = (bf16[384,128]{1,0:T(8,128)(2,1)S(1)}, bf16[384,128]{1,0:T(8,128)(2,1)}, u32[]{:S(2)}) copy-start(bf16[384,128]{1,0:T(8,128)(2,1)} %copy-done.3) | copy-start | bytes 294916
  60.0 1.4 %copy-start.6 = (bf16[384,128]{1,0:T(8,128)(2,1)S(1)}, bf16[384,128]{1,0:T(8,128)(2,1)}, u32[]{:S(2)}) copy-start(bf16[384,128]{1,0:T(8,128)(2,1)} %copy-done.5) | copy-start | bytes 294916
  61.2 0.9 copy-start.8
  62.5 6.0 %collective-permute-start.7 = (bf16[256,256]{1,0:T(8,128)(2,1)S(1)}, bf16[256,256]{1,0:T(8,128)(2,1)S(1)}, u32[]{:S(2)}, u32[]{:S(2)}) collective-permute-start(bf16[256,256]{1,0:T(8,128)(2,1)S(1)} %get-tuple-element.21), channel_id=1, source_target_pairs={{0,48},{16,0},{32,16},{48,32},{1,49},{17,1},{33,17},{49,33},{2,50}... | collective-permute-start | bytes 393224 | tf_op jit(solution)/shard_map/ppermute | solution.py:75
  62.6 9.4 %collective-permute-start.14 = (bf16[256,256]{1,0:T(8,128)(2,1)S(1)}, bf16[256,256]{1,0:T(8,128)(2,1)S(1)}, u32[]{:S(2)}, u32[]{:S(2)}) collective-permute-start(bf16[256,256]{1,0:T(8,128)(2,1)S(1)} %get-tuple-element.21), channel_id=1, source_target_pairs={{0,128},{64,192},{128,0},{192,64},{1,129},{65,193},{129,1},{193,65... | collective-permute-start | bytes 393224 | tf_op jit(solution)/shard_map/ppermute | solution.py:176
  63.5 7.5 %collective-permute-start.8 = (bf16[256,256]{1,0:T(8,128)(2,1)S(1)}, bf16[256,256]{1,0:T(8,128)(2,1)S(1)}, u32[]{:S(2)}, u32[]{:S(2)}) collective-permute-start(bf16[256,256]{1,0:T(8,128)(2,1)S(1)} %get-tuple-element.21), channel_id=1, source_target_pairs={{0,32},{16,48},{32,0},{48,16},{1,33},{17,49},{33,1},{49,17},{2,34}... | collective-permute-start | bytes 393224 | tf_op jit(solution)/shard_map/ppermute | solution.py:75
  63.7 8.2 %collective-permute-start.9 = (bf16[256,256]{1,0:T(8,128)(2,1)S(1)}, bf16[256,256]{1,0:T(8,128)(2,1)S(1)}, u32[]{:S(2)}, u32[]{:S(2)}) collective-permute-start(bf16[256,256]{1,0:T(8,128)(2,1)S(1)} %get-tuple-element.21), channel_id=1, source_target_pairs={{0,16},{16,32},{32,48},{48,0},{1,17},{17,33},{33,49},{49,1},{2,18}... | collective-permute-start | bytes 393224 | tf_op jit(solution)/shard_map/ppermute | solution.py:75
  72.0 1.0 copy-start.11
  73.7 19.1 %copy-start.9 = (bf16[4,256,384]{1,2,0:T(8,128)(2,1)S(1)}, bf16[4,256,384]{1,2,0:T(8,128)(2,1)}, u32[]{:S(2)}) copy-start(bf16[4,256,384]{1,2,0:T(8,128)(2,1)} %copy-done.8) | copy-start | bytes 2359300
  75.0 2.6 %collective-permute-start.10 = (f32[256,16]{0,1:T(8,128)S(1)}, f32[256,16]{0,1:T(8,128)S(1)}, u32[]{:S(2)}, u32[]{:S(2)}) collective-permute-start(f32[256,16]{0,1:T(8,128)S(1)} %select_reduce_fusion), channel_id=1, source_target_pairs={{0,0},{16,64},{32,128},{48,192},{64,16},{80,80},{96,144},{112,208}... | collective-permute-start | bytes 49160 | tf_op jit(solution)/shard_map/ppermute | solution.py:158
  77.6 12.9 %collective-permute-start.11 = (f32[256,16]{0,1:T(8,128)S(1)}, f32[256,16]{0,1:T(8,128)S(1)}, u32[]{:S(2)}, u32[]{:S(2)}) collective-permute-start(f32[256,16]{0,1:T(8,128)S(1)} %collective-permute-done.10), channel_id=1, source_target_pairs={{0,192},{64,0},{128,64},{192,128},{1,193},{65,1},{129,65},{193,129... | collective-permute-start | bytes 49160 | tf_op jit(solution)/shard_map/ppermute | solution.py:75
  85.1 5.3 %collective-permute-start.12 = (f32[256,16]{0,1:T(8,128)S(1)}, f32[256,16]{0,1:T(8,128)S(1)}, u32[]{:S(2)}, u32[]{:S(2)}) collective-permute-start(f32[256,16]{0,1:T(8,128)S(1)} %collective-permute-done.10), channel_id=1, source_target_pairs={{0,128},{64,192},{128,0},{192,64},{1,129},{65,193},{129,1},{193,65... | collective-permute-start | bytes 49160 | tf_op jit(solution)/shard_map/ppermute | solution.py:75
  87.4 5.0 %collective-permute-start.13 = (f32[256,16]{0,1:T(8,128)S(1)}, f32[256,16]{0,1:T(8,128)S(1)}, u32[]{:S(2)}, u32[]{:S(2)}) collective-permute-start(f32[256,16]{0,1:T(8,128)S(1)} %collective-permute-done.10), channel_id=1, source_target_pairs={{0,64},{64,128},{128,192},{192,0},{1,65},{65,129},{129,193},{193,1... | collective-permute-start | bytes 49160 | tf_op jit(solution)/shard_map/ppermute | solution.py:75
  92.8 2.4 %copy-start.10 = (bf16[4,256,256]{2,1,0:T(8,128)(2,1)S(1)}, bf16[4,256,256]{2,1,0:T(8,128)(2,1)}, u32[]{:S(2)}) copy-start(bf16[4,256,256]{2,1,0:T(8,128)(2,1)} %constant_dynamic-slice_fusion) | copy-start | bytes 1572868
